TPU v7x, 128 devices: a whole 4x4x4 slice. The times are simulated.
128 devices in a mesh: req: 32 (over z, x, core), tok: 4 (over y).
Axes of the slice: x: 4, y: 4, z: 4, core: 2. Of those that a mesh axis runs over, the one named last changes fastest.
Arguments:
- tokens: bfloat16 [32768, 1280], P(('req', 'tok')), may hold values from -6 to 6
- segments: int32 [32, 1024], P('req'), may hold values from 0 to 16, as said below
- gain_attn: float32 [1280], replicated, may hold values from 0.1 to 1.9
- w_qkv: bfloat16 [1280, 3, 1280], P(None, None, 'tok'), may hold values from -1 to 1
- w_out: bfloat16 [1280, 1280], P('tok'), may hold values from -0.15625 to 0.15625
- gain_mlp: float32 [1280], replicated, may hold values from 0.1 to 1.9
- w_up: bfloat16 [1280, 5120], P(None, ('req', 'tok')), may hold values from -0.15625 to 0.15625
- w_down_t: bfloat16 [1280, 5120], P(None, ('req', 'tok')), may hold values from -0.078125 to 0.078125
- gain_merge: float32 [1280], replicated, may hold values from 0.1 to 1.9
- w_proj: bfloat16 [5120, 4096], P(None, 'tok'), may hold values from -0.078125 to 0.078125
Outputs:
- owned: bfloat16 [8192, 4096], P('req', 'tok')
Inputs may be any that keep to these rules, and one draw needn't show every extreme that they name: `segments`: in each row segment ids start at 0 and never fall; every image covers whole aligned runs of 4 positions and at most 512 positions; image 0 of every row covers exactly 512, and every row holds exactly max(1, 16) + 1 images.
All inputs are finite; a program needn't handle non-finite values.
Results may differ from a plain program's by a relative error of at most 0.015.
The roundings to bfloat16 on the way count: a program that leaves them out, or rounds other values in their place, can miss the bound.
Values may be sent and summed in bfloat16 or wider, within the bound.
No kernel may reach another device: no remote copies, remote signals or barrier semaphores. Data moves between devices by JAX's collectives and lax.ppermute only.
A program may use at most 128 MiB of HBM per device.

v0:
```python
import math

import jax
import jax.numpy as jnp
from jax import lax
from jax.sharding import Mesh, PartitionSpec as P


HDIM = 80


def layer_norm(values, gain):
    mean = jnp.mean(values, axis=-1, keepdims=True)
    centered = values - mean
    spread = jnp.mean(centered * centered, axis=-1, keepdims=True)
    return centered * lax.rsqrt(spread + 1e-06) * gain


def hidden_fold(rows, pieces):
    up_piece, down_piece = pieces
    hidden = jax.nn.gelu(
        jnp.dot(rows, up_piece, preferred_element_type=jnp.float32), approximate=False
    ).astype(jnp.bfloat16)
    return lax.dot_general(
        hidden, down_piece, (((1,), (1,)), ((), ())), preferred_element_type=jnp.float32
    )


def permute_gather(rows, axis):
    count = lax.axis_size(axis)
    here = lax.axis_index(axis)
    shifted = [rows] + [
        lax.ppermute(rows, axis, [(i, (i + s) % count) for i in range(count)])
        for s in range(1, count)
    ]
    stacked = jnp.stack(shifted)
    blocks = [
        lax.dynamic_index_in_dim(stacked, (here - source) % count, axis=0, keepdims=False)
        for source in range(count)
    ]
    return jnp.concatenate(blocks, axis=0)


def permute_scatter(parts, axis):
    count = lax.axis_size(axis)
    here = lax.axis_index(axis)
    blocks = parts.reshape(count, parts.shape[0] // count, parts.shape[1])
    total = lax.dynamic_index_in_dim(blocks, here, axis=0, keepdims=False).astype(jnp.float32)
    for s in range(1, count):
        outgoing = lax.dynamic_index_in_dim(blocks, (here + s) % count, axis=0, keepdims=False)
        incoming = lax.ppermute(outgoing, axis, [(i, (i + s) % count) for i in range(count)])
        total = total + incoming.astype(jnp.float32)
    return total


def attend_block(
    queries,
    keys_blocked,
    values_blocked,
    images,
    images_blocked,
    first_row,
    q_block,
    k_block,
    scale,
):
    local_heads = keys_blocked.shape[2]
    query_part = queries[first_row : first_row + q_block].reshape(q_block, local_heads, HDIM)
    query_images = images[first_row : first_row + q_block]
    key_first = jnp.sum((images < images[first_row]).astype(jnp.int32))
    key_last = jnp.sum((images <= images[first_row + q_block - 1]).astype(jnp.int32))
    block_first = key_first // k_block
    block_last = (key_last + k_block - 1) // k_block

    def block_scores(kblock):
        scores = (
            jnp.einsum(
                "qhd,khd->hqk", query_part, keys_blocked[kblock], preferred_element_type=jnp.float32
            )
            * scale
        )
        same = query_images[:, None] == images_blocked[kblock][None, :]
        return jnp.where(same[None], scores, -1e30)

    def scan_stats(kblock, carry):
        row_max, row_sum = carry
        scores = block_scores(kblock)
        new_max = jnp.maximum(row_max, jnp.max(scores, axis=-1))
        row_sum = row_sum * jnp.exp(row_max - new_max) + jnp.sum(
            jnp.exp(scores - new_max[..., None]), axis=-1
        )
        return (new_max, row_sum)

    start_max = jnp.full((local_heads, q_block), -1e30, jnp.float32)
    start_sum = jnp.zeros((local_heads, q_block), jnp.float32)
    row_max, row_sum = lax.fori_loop(block_first, block_last, scan_stats, (start_max, start_sum))

    def add_values(kblock, totals):
        scores = block_scores(kblock)
        weights = (jnp.exp(scores - row_max[..., None]) / row_sum[..., None]).astype(jnp.bfloat16)
        return totals + jnp.einsum(
            "hqk,khd->qhd", weights, values_blocked[kblock], preferred_element_type=jnp.float32
        )

    totals = lax.fori_loop(
        block_first, block_last, add_values, jnp.zeros((q_block, local_heads, HDIM), jnp.float32)
    )
    return totals.reshape(q_block, local_heads * HDIM).astype(jnp.bfloat16)


def layer(tokens, segments, gain_attn, w_qkv, w_out, gain_mlp, w_up, w_down_t, gain_merge, w_proj):
    both = lax.all_gather(jnp.stack([w_up, w_down_t]), ("zx", "tok"), axis=2, tiled=True)
    up_full, down_full = both[0], both[1]
    inputs = tokens.astype(jnp.float32)
    normed = layer_norm(inputs, gain_attn).astype(jnp.bfloat16)
    local_width = w_qkv.shape[2]
    joined = w_qkv.reshape(w_qkv.shape[0], 3 * local_width)
    stacked = jnp.dot(
        permute_gather(normed, "tok"),
        joined,
        preferred_element_type=jnp.float32,
    ).astype(jnp.bfloat16)
    group = stacked.shape[0]
    local_heads = local_width // HDIM
    q_block = min(512, group)
    k_block = min(128, group)
    scale = 1.0 / math.sqrt(HDIM)
    queries = stacked[:, :local_width]
    keys_blocked = stacked[:, local_width : 2 * local_width].reshape(
        group // k_block, k_block, local_heads, HDIM
    )
    values_blocked = stacked[:, 2 * local_width :].reshape(
        group // k_block, k_block, local_heads, HDIM
    )
    images = segments[0]
    images_blocked = images.reshape(group // k_block, k_block)
    outputs = []
    for block in range(group // q_block):
        outputs.append(
            attend_block(
                queries,
                keys_blocked,
                values_blocked,
                images,
                images_blocked,
                block * q_block,
                q_block,
                k_block,
                scale,
            )
        )
    heads_out = jnp.concatenate(outputs, axis=0)
    attended = permute_scatter(
        jnp.dot(heads_out, w_out, preferred_element_type=jnp.float32).astype(jnp.bfloat16),
        "tok",
    )
    first = (inputs + attended).astype(jnp.bfloat16)
    normed_mlp = layer_norm(first.astype(jnp.float32), gain_mlp).astype(jnp.bfloat16)
    mlp_out = permute_scatter(
        hidden_fold(permute_gather(normed_mlp, "core"), (up_full, down_full)), "core"
    )
    second = first.astype(jnp.float32) + mlp_out
    normed_merge = layer_norm(second, gain_merge).astype(jnp.bfloat16)
    merged = normed_merge.reshape(inputs.shape[0] // 4, 4 * inputs.shape[1])
    projected = jnp.dot(
        lax.all_gather(merged, "tok", axis=0, tiled=True),
        w_proj,
        preferred_element_type=jnp.float32,
    ).astype(jnp.bfloat16)
    return lax.all_to_all(projected, ("zx", "core"), split_axis=0, concat_axis=0, tiled=True)


def solution(mesh):
    devices = mesh.devices
    split = Mesh(devices.reshape(devices.shape[0] // 2, 2, devices.shape[1]), ("zx", "core", "tok"))
    rows = ("zx", "core")
    return jax.shard_map(
        layer,
        mesh=split,
        in_specs=(
            P(rows + ("tok",), None),
            P(rows, None),
            P(),
            P(None, None, "tok"),
            P("tok", None),
            P(),
            P(None, rows + ("tok",)),
            P(None, rows + ("tok",)),
            P(),
            P(None, "tok"),
        ),
        out_specs=P(rows, "tok"),
        check_vma=False,
    )
```

profile of v0, /device:TPU:1, one launch (start us, length us, event | category | flops | bytes accessed | tf_op | source)
XLA Modules:
  0.0 326.7 jit_solution(15843053066475194939)
XLA Ops:
  6.6 1.1 pad_maximum_fusion.1
  8.6 1.3 convert_reduce_fusion.1
  9.9 1.4 fusion.88
  11.3 1.8 fusion.90
  13.1 3.6 %collective-permute-start.2 = (bf16[256,1280]{1,0:T(8,128)(2,1)}, bf16[256,1280]{1,0:T(8,128)(2,1)}, u32[]{:S(2)}, u32[]{:S(2)}) collective-permute-start(bf16[256,1280]{1,0:T(8,128)(2,1)} %fusion.90), channel_id=1, source_target_pairs={{0,3},{1,0},{2,1},{3,2},{4,7},{5,4},{6,5},{7,6},{8,11},{9,8},{10,9... | collective-permute-start | bytes 1966088 | tf_op jit(solution)/shard_map/ppermute | solution.py:33
  18.4 3.3 fusion.110
  28.7 3.6 %collective-permute-done.2 = bf16[256,1280]{1,0:T(8,128)(2,1)} collective-permute-done((bf16[256,1280]{1,0:T(8,128)(2,1)}, bf16[256,1280]{1,0:T(8,128)(2,1)}, u32[]{:S(2)}, u32[]{:S(2)}) %collective-permute-start.2) | collective-permute-done | bytes 655392 | tf_op jit(solution)/shard_map/ppermute | solution.py:33
  32.2 2.6 collective-permute-done.1
  34.8 16.5 %collective-permute-done = bf16[256,1280]{1,0:T(8,128)(2,1)} collective-permute-done((bf16[256,1280]{1,0:T(8,128)(2,1)}, bf16[256,1280]{1,0:T(8,128)(2,1)}, u32[]{:S(2)}, u32[]{:S(2)}) %collective-permute-start) | collective-permute-done | bytes 655392 | tf_op jit(solution)/shard_map/ppermute | solution.py:33
  51.3 1.8 pad_maximum_fusion
  53.3 2.7 fusion.78
  57.6 3.0 while.46
  60.7 7.0 %while.47 = (s32[]{:T(128)}, f32[512,4,80]{0,2,1:T(8,128)S(1)}, s32[]{:T(128)}, bf16[8,128,4,80]{1,3,2,0:T(8,128)(2,1)}, s32[512]{0:T(512)S(1)}, /*index=5*/s32[...) while((s32[]{:T(128)}, f32[512,4,80]{0,2,1:T(8,128)S(1)}, ...), condition=%wide.region_17.18_spmd, body=%wide.region_16.17_spmd.sunk | while | flops 85426176 | bytes 1954475 | solution.py:105
  60.9 1.6 fusion.162
  62.6 1.6 fusion.162
  64.3 1.6 fusion.162
  66.1 1.6 fusion.162
  67.8 3.1 while.44
  70.9 7.0 %while.45 = (s32[]{:T(128)}, f32[512,4,80]{0,2,1:T(8,128)S(1)}, s32[]{:T(128)}, bf16[8,128,4,80]{1,3,2,0:T(8,128)(2,1)}, s32[512]{0:T(512)S(1)}, /*index=5*/s32[...) while((s32[]{:T(128)}, f32[512,4,80]{0,2,1:T(8,128)S(1)}, ...), condition=%wide.region_9.10_spmd, body=%wide.region_8.9_spmd.sunk | while | flops 85426176 | bytes 1954475 | solution.py:105
  71.1 1.6 fusion.155
  72.8 1.6 fusion.155
  74.5 1.6 fusion.155
  76.3 1.6 fusion.155
  77.9 2.7 convolution_convert_fusion
  80.7 1.5 copy-done.4
  82.1 1.2 dynamic-slice_bitcast_fusion.5
  83.8 1.0 collective-permute-start.3
  84.8 29.0 %collective-permute-done.5 = bf16[256,1280]{1,0:T(8,128)(2,1)S(1)} collective-permute-done((bf16[256,1280]{1,0:T(8,128)(2,1)}, bf16[256,1280]{1,0:T(8,128)(2,1)S(1)}, u32[]{:S(2)}, u32[]{:S(2)}) %collective-permute-start.5) | collective-permute-done | bytes 655392 | tf_op jit(solution)/shard_map/ppermute | solution.py:51
  113.8 1.2 collective-permute-done.4
  115.0 23.8 %collective-permute-done.3 = bf16[256,1280]{1,0:T(8,128)(2,1)} collective-permute-done((bf16[256,1280]{1,0:T(8,128)(2,1)S(1)}, bf16[256,1280]{1,0:T(8,128)(2,1)}, u32[]{:S(2)}, u32[]{:S(2)}) %collective-permute-start.3) | collective-permute-done | bytes 655392 | tf_op jit(solution)/shard_map/ppermute | solution.py:51
  138.8 1.8 convert_reduce_fusion
  141.3 2.4 collective-permute-start.6
  143.9 1.5 collective-permute-done.6
  145.4 1.3 fusion.105
  146.6 3.2 all-gather.3.cloned.1.call-done
  149.8 25.6 %fusion.120 = (bf16[1,1280,2560]{1,0,2:T(2,128)(2,1)}, bf16[1,1280,2560]{1,0,2:T(2,128)(2,1)}) fusion(bf16[2,1280,2560]{1,0,2:T(2,128)(2,1)} %all-gather.3.cloned.1.call-done), kind=kLoop, calls=%fused_computation.172 | loop fusion | bytes 26214400 | tf_op jit(solution)/shard_map/slice | solution.py:113
  175.4 26.0 %copy.44 = bf16[1,1280,2560]{2,1,0:T(8,128)(2,1)} copy(bf16[1,1280,2560]{1,0,2:T(2,128)(2,1)} %get-tuple-element.398) | data formatting | bytes 13107200
  201.5 26.1 %copy.45 = bf16[1,1280,2560]{2,1,0:T(8,128)(2,1)} copy(bf16[1,1280,2560]{1,0,2:T(2,128)(2,1)} %get-tuple-element.397) | data formatting | bytes 13107200
  227.6 16.1 %fusion.62 = bf16[512,2560]{1,0:T(8,128)(2,1)S(1)} fusion(bf16[1,1280,2560]{2,1,0:T(8,128)(2,1)} %copy.44, bf16[256,1280]{1,0:T(8,128)(2,1)S(1)} %copy-done.6, bf16[256,1280]{1,0:T(8,128)(2,1)S(1)} %get-tuple-element.410), kind=kOutput, calls=%fused_computation.75 | convolution fusion | flops 3443261440 | bytes 10485760 | tf_op jit(solution)/shard_map/dot_general | solution.py:22
  243.6 3.6 %fusion.56 = f32[2,256,1280]{2,1,0:T(8,128)S(1)} fusion(bf16[2,256,2560]{2,1,0:T(8,128)(2,1)S(1)} %bitcast.214, bf16[1,1280,2560]{2,1,0:T(8,128)(2,1)S(1)} %copy-done.3), kind=kOutput, calls=%fused_computation.69 | convolution fusion | flops 3355443200 | bytes 11796480 | tf_op jit(solution)/shard_map/dot_general | solution.py:24
  247.2 1.5 copy-done.5
  248.8 1.1 collective-permute-start.7
  250.0 2.8 collective-permute-done.7
  252.8 2.0 fusion.116
  255.3 1.2 reshape.216
  256.6 35.7 %all-gather.5.cloned.1.call-done = bf16[256,5120]{1,0:T(8,128)(2,1)} async-done(((bf16[64,5120]{1,0:T(8,128)(2,1)}), bf16[256,5120]{1,0:T(8,128)(2,1)}) %all-gather.5.cloned.1.call-update) | async-done | bytes 2621456 | tf_op jit(solution)/shard_map/all_gather | solution.py:166
  292.2 7.8 %fusion.101 = bf16[32,8,1024]{2,1,0:T(8,128)(2,1)S(1)} fusion(bf16[256,5120]{1,0:T(8,128)(2,1)} %all-gather.5.cloned.1.call-done, bf16[5120,1024]{1,0:T(8,128)(2,1)} %param.27), kind=kOutput, calls=%fused_computation.134 | convolution fusion | flops 2684616704 | bytes 13631488 | tf_op jit(solution)/shard_map/dot_general | solution.py:165
  300.0 19.1 %all_to_all.12 = bf16[32,8,1024]{2,1,0:T(8,128)(2,1)S(1)} all-to-all(bf16[32,8,1024]{2,1,0:T(8,128)(2,1)S(1)} %fusion.101), channel_id=1, replica_groups=mesh['zx'=16,'core'=2,'tok'=4] {'zx','core'}, dimensions={0} | all-to-all | bytes 1048576 | tf_op jit(solution)/shard_map/all_to_all | solution.py:170
  (132 shorter events, 14.0 us)
Async XLA Ops:
  6.5 46.8 %copy-start = (bf16[1280,3,320]{0,2,1:T(8,128)(2,1)S(1)}, bf16[1280,3,320]{0,2,1:T(8,128)(2,1)}, u32[]{:S(2)}) copy-start(bf16[1280,3,320]{0,2,1:T(8,128)(2,1)} %param.21) | copy-start | bytes 7372804
  6.5 4.8 %copy-start.2 = (bf16[256,1280]{1,0:T(8,128)(2,1)S(1)}, bf16[256,1280]{1,0:T(8,128)(2,1)}, u32[]{:S(2)}) copy-start(bf16[256,1280]{1,0:T(8,128)(2,1)} %param.18) | copy-start | bytes 1966084
  6.5 21.8 %copy-start.7 = (f32[1280]{0:T(1024)S(1)}, f32[1280]{0:T(1024)}, u32[]{:S(2)}) copy-start(f32[1280]{0:T(1024)} %param.20) | copy-start | bytes 15364
  6.5 11.2 %copy-start.9 = (s32[1,1024]{1,0:T(1,128)S(1)}, s32[1,1024]{1,0:T(1,128)}, u32[]{:S(2)}) copy-start(s32[1,1024]{1,0:T(1,128)} %param.19) | copy-start | bytes 12292
  6.5 143.3 %all-gather.3.cloned.1.call-start = ((), (), s32[]{:S(2)}) async-start(), calls=%async_computation.1 | async-start | bytes 13312000 | tf_op jit(solution)/shard_map/all_gather | solution.py:112
  8.6 283.7 %all-gather.5.cloned.1.call-start = ((), (), s32[]{:S(2)}) async-start(), calls=%async_computation.2 | async-start | bytes 3276800 | tf_op jit(solution)/shard_map/all_gather | solution.py:166
  13.1 19.1 %collective-permute-start.2 = (bf16[256,1280]{1,0:T(8,128)(2,1)}, bf16[256,1280]{1,0:T(8,128)(2,1)}, u32[]{:S(2)}, u32[]{:S(2)}) collective-permute-start(bf16[256,1280]{1,0:T(8,128)(2,1)} %fusion.90), channel_id=1, source_target_pairs={{0,3},{1,0},{2,1},{3,2},{4,7},{5,4},{6,5},{7,6},{8,11},{9,8},{10,9... | collective-permute-start | bytes 1966088 | tf_op jit(solution)/shard_map/ppermute | solution.py:33
  16.7 18.1 %collective-permute-start.1 = (bf16[256,1280]{1,0:T(8,128)(2,1)}, bf16[256,1280]{1,0:T(8,128)(2,1)}, u32[]{:S(2)}, u32[]{:S(2)}) collective-permute-start(bf16[256,1280]{1,0:T(8,128)(2,1)} %fusion.90), channel_id=1, source_target_pairs={{0,2},{1,3},{2,0},{3,1},{4,6},{5,7},{6,4},{7,5},{8,10},{9,11},{10,... | collective-permute-start | bytes 1966088 | tf_op jit(solution)/shard_map/ppermute | solution.py:33
  17.1 34.3 %collective-permute-start = (bf16[256,1280]{1,0:T(8,128)(2,1)}, bf16[256,1280]{1,0:T(8,128)(2,1)}, u32[]{:S(2)}, u32[]{:S(2)}) collective-permute-start(bf16[256,1280]{1,0:T(8,128)(2,1)} %fusion.90), channel_id=1, source_target_pairs={{0,1},{1,2},{2,3},{3,0},{4,5},{5,6},{6,7},{7,4},{8,9},{9,10},{10,1... | collective-permute-start | bytes 1966088 | tf_op jit(solution)/shard_map/ppermute | solution.py:33
  80.6 1.5 copy-start.4
  83.3 57.6 %copy-start.8 = (f32[1280]{0:T(1024)S(1)}, f32[1280]{0:T(1024)}, u32[]{:S(2)}) copy-start(f32[1280]{0:T(1024)} %param.23) | copy-start | bytes 15364
  83.3 30.5 %collective-permute-start.5 = (bf16[256,1280]{1,0:T(8,128)(2,1)}, bf16[256,1280]{1,0:T(8,128)(2,1)S(1)}, u32[]{:S(2)}, u32[]{:S(2)}) collective-permute-start(bf16[256,1280]{1,0:T(8,128)(2,1)} %get-tuple-element.400), channel_id=1, source_target_pairs={{0,3},{1,0},{2,1},{3,2},{4,7},{5,4},{6,5},{7,6},{8,11},{9,8},{10,9... | collective-permute-start | bytes 1966088 | tf_op jit(solution)/shard_map/ppermute | solution.py:51
  83.3 31.6 %collective-permute-start.4 = (bf16[256,1280]{1,0:T(8,128)(2,1)}, bf16[256,1280]{1,0:T(8,128)(2,1)S(1)}, u32[]{:S(2)}, u32[]{:S(2)}) collective-permute-start(bf16[256,1280]{1,0:T(8,128)(2,1)} %get-tuple-element.401), channel_id=1, source_target_pairs={{0,2},{1,3},{2,0},{3,1},{4,6},{5,7},{6,4},{7,5},{8,10},{9,11},{10,... | collective-permute-start | bytes 1966088 | tf_op jit(solution)/shard_map/ppermute | solution.py:51
  83.8 55.0 %collective-permute-start.3 = (bf16[256,1280]{1,0:T(8,128)(2,1)S(1)}, bf16[256,1280]{1,0:T(8,128)(2,1)}, u32[]{:S(2)}, u32[]{:S(2)}) collective-permute-start(bf16[256,1280]{1,0:T(8,128)(2,1)S(1)} %get-tuple-element.399), channel_id=1, source_target_pairs={{0,1},{1,2},{2,3},{3,0},{4,5},{5,6},{6,7},{7,4},{8,9},{9,10},{10,1... | collective-permute-start | bytes 1966088 | tf_op jit(solution)/shard_map/ppermute | solution.py:51
  141.3 4.1 %collective-permute-start.6 = (bf16[256,1280]{1,0:T(8,128)(2,1)S(1)}, bf16[256,1280]{1,0:T(8,128)(2,1)S(1)}, u32[]{:S(2)}, u32[]{:S(2)}) collective-permute-start(bf16[256,1280]{1,0:T(8,128)(2,1)S(1)} %fusion.87), channel_id=1, source_target_pairs={{0,4},{4,0},{1,5},{5,1},{2,6},{6,2},{3,7},{7,3},{8,12},{12,8},{9,1... | collective-permute-start | bytes 1966088 | tf_op jit(solution)/shard_map/ppermute | solution.py:33
  201.5 26.1 %copy-start.6 = (bf16[256,1280]{1,0:T(8,128)(2,1)S(1)}, bf16[256,1280]{1,0:T(8,128)(2,1)}, u32[]{:S(2)}) copy-start(bf16[256,1280]{1,0:T(8,128)(2,1)} %get-tuple-element.411) | copy-start | bytes 1966084
  227.5 16.1 %copy-start.3 = (bf16[1,1280,2560]{2,1,0:T(8,128)(2,1)S(1)}, bf16[1,1280,2560]{2,1,0:T(8,128)(2,1)}, u32[]{:S(2)}) copy-start(bf16[1,1280,2560]{2,1,0:T(8,128)(2,1)} %copy.45) | copy-start | bytes 19660804
  247.2 1.5 copy-start.5
  248.8 3.9 %collective-permute-start.7 = (f32[256,1280]{1,0:T(8,128)S(1)}, f32[256,1280]{1,0:T(8,128)}, u32[]{:S(2)}, u32[]{:S(2)}) collective-permute-start(f32[256,1280]{1,0:T(8,128)S(1)} %dynamic-slice_bitcast_fusion.2), channel_id=1, source_target_pairs={{0,4},{4,0},{1,5},{5,1},{2,6},{6,2},{3,7},{7,3},{8,12},{12,8},{9,1... | collective-permute-start | bytes 3932168 | tf_op jit(solution)/shard_map/ppermute | solution.py:51
  250.0 5.1 %copy-start.10 = (f32[1280]{0:T(1024)S(1)}, f32[1280]{0:T(1024)}, u32[]{:S(2)}) copy-start(f32[1280]{0:T(1024)} %param.26) | copy-start | bytes 15364
  292.2 27.7 %copy-start.1 = (bf16[1280,3,320]{0,2,1:T(8,128)(2,1)S(1)}, bf16[1280,3,320]{0,2,1:T(8,128)(2,1)}, u32[]{:S(2)}) copy-start(bf16[1280,3,320]{0,2,1:T(8,128)(2,1)} %param.21) | copy-start | bytes 7372804
Sparse Core Ops, SparseCore 0:
  10.2 139.5 all-gather.2
  256.7 35.4 all-gather.4
where the time goes:
time: 329 us; the launch traced here: 327 us
  waiting for transfers between devices  120 us (36%)
  local copies, waits for them, and re-layouts  87.5 us (27%)
  matrix products  48.7 us (15%)
  other arithmetic  20.7 us (6%)
  between operations  20.5 us (6%)
  blocking collectives  19.1 us (6%)
  starting transfers between devices  9.64 us (3%)
    ppermute x4, waiting for transfers between devices, permute_scatter(): lax.ppermute(outgoing, axis, [(i, (i + s) % count) for i in range(count)])  56.8 us
    unnamed x28, local copies, waits for them, and re-layouts  56.2 us
    all_gather x1, waiting for transfers between devices, layer(): lax.all_gather(merged, 'tok', axis=0, tiled=True)  35.7 us
    slice x1, local copies, waits for them, and re-layouts, layer(): up_full, down_full = (both[0], both[1])  25.6 us
    ppermute x4, waiting for transfers between devices, permute_gather(): lax.ppermute(rows, axis, [(i, (i + s) % count) for i in range(count)])  24.1 us
    all_to_all x1, blocking collectives, layer(): lax.all_to_all(projected, ('zx', 'core'), split_axis=0, concat_axis=0, ti...  19.1 us
    dot_general x1, matrix products, hidden_fold(): jnp.dot(rows, up_piece, preferred_element_type=jnp.float32)  16.1 us
    dot_general x8, matrix products, add_values(): jnp.einsum('hqk,khd->qhd', weights, values_blocked[kblock], preferred_ele...  12.7 us
  transfers between devices with their start and end apart: 10, of which 10 were waited for; matrix products, arithmetic and copies ran while one was open for 13% of the time, Pallas kernels for 0%

commit v1 on v0

--- a/solution.py
+++ b/solution.py
@@ -109,7 +109,7 @@
 
 
 def layer(tokens, segments, gain_attn, w_qkv, w_out, gain_mlp, w_up, w_down_t, gain_merge, w_proj):
-    both = lax.all_gather(jnp.stack([w_up, w_down_t]), ("zx", "tok"), axis=2, tiled=True)
+    both = lax.all_gather(jnp.stack([w_up, w_down_t]), ("zx", "core", "tok"), axis=2, tiled=True)
     up_full, down_full = both[0], both[1]
     inputs = tokens.astype(jnp.float32)
     normed = layer_norm(inputs, gain_attn).astype(jnp.bfloat16)
@@ -156,14 +156,12 @@
     )
     first = (inputs + attended).astype(jnp.bfloat16)
     normed_mlp = layer_norm(first.astype(jnp.float32), gain_mlp).astype(jnp.bfloat16)
-    mlp_out = permute_scatter(
-        hidden_fold(permute_gather(normed_mlp, "core"), (up_full, down_full)), "core"
-    )
+    mlp_out = hidden_fold(normed_mlp, (up_full, down_full))
     second = first.astype(jnp.float32) + mlp_out
     normed_merge = layer_norm(second, gain_merge).astype(jnp.bfloat16)
     merged = normed_merge.reshape(inputs.shape[0] // 4, 4 * inputs.shape[1])
     projected = jnp.dot(
-        lax.all_gather(merged, "tok", axis=0, tiled=True),
+        permute_gather(merged, "tok"),
         w_proj,
         preferred_element_type=jnp.float32,
     ).astype(jnp.bfloat16)

time: 329 us -> 248 us (0.75)
  local copies, waits for them, and re-layouts: 87.5 us -> 23.5 us
  waiting for transfers between devices: 120 us -> 83.7 us
  matrix products: 48.7 us -> 56.5 us
  other arithmetic: 20.7 us -> 28.4 us
    unnamed x28 -> x18, local copies, waits for them, and re-layouts: 56.2 us -> 2.18 us
    all_gather x2 -> x1, waiting for transfers between devices: 38.9 us -> 0.02 us  [layer(): lax.all_gather(jnp.stack([w_up, w_down_t]), ('zx', 'core', 'tok'), axis=2...]
    slice x1 -> x0, local copies, waits for them, and re-layouts: 25.6 us -> none  [layer(): up_full, down_full = (both[0], both[1])]
    dot_general x1, matrix products: 3.58 us -> 25.7 us  [hidden_fold(): lax.dot_general(hidden, down_piece, (((1,), (1,)), ((), ())), preferred_e...]
    ppermute x4 -> x6, waiting for transfers between devices: 24.1 us -> 43.2 us  [permute_gather(): lax.ppermute(rows, axis, [(i, (i + s) % count) for i in range(count)])]
    dot_general x2 -> x1, matrix products: 23.9 us -> 7.06 us  [layer(): jnp.dot(permute_gather(merged, 'tok'), w_proj, preferred_element_type=jnp...]
    ppermute x4 -> x3, waiting for transfers between devices: 56.8 us -> 40.5 us  [permute_scatter(): lax.ppermute(outgoing, axis, [(i, (i + s) % count) for i in range(count)])]
    dynamic_slice x16, local copies, waits for them, and re-layouts: 0.13 us -> 11.2 us  [block_scores(): same = query_images[:, None] == images_blocked[kblock][None, :]]
  transfers between devices with their start and end apart: 10 -> 10, of which waited for: 10 -> 5; matrix products, arithmetic and copies ran while one was open for 13% -> 28% of each run, Pallas kernels for 0% -> 0%
where the time goes in v1:
time: 248 us; the launch traced here: 246 us
  waiting for transfers between devices  83.7 us (34%)
  matrix products  56.5 us (23%)
  other arithmetic  28.4 us (11%)
  local copies, waits for them, and re-layouts  23.5 us (9%)
  between operations  20.5 us (8%)
  blocking collectives  20 us (8%)
  starting transfers between devices  12.5 us (5%)
    ppermute x6, waiting for transfers between devices, permute_gather(): lax.ppermute(rows, axis, [(i, (i + s) % count) for i in range(count)])  43.2 us
    ppermute x3, waiting for transfers between devices, permute_scatter(): lax.ppermute(outgoing, axis, [(i, (i + s) % count) for i in range(count)])  40.5 us
    dot_general x1, matrix products, hidden_fold(): lax.dot_general(hidden, down_piece, (((1,), (1,)), ((), ())), preferred_e...  25.7 us
    all_to_all x1, blocking collectives, layer(): lax.all_to_all(projected, ('zx', 'core'), split_axis=0, concat_axis=0, ti...  20 us
    dot_general x8, matrix products, add_values(): jnp.einsum('hqk,khd->qhd', weights, values_blocked[kblock], preferred_ele...  14.9 us
    dynamic_slice x16, local copies, waits for them, and re-layouts, block_scores(): same = query_images[:, None] == images_blocked[kblock][None, :]  11.2 us
    ppermute x6, starting transfers between devices, permute_gather(): lax.ppermute(rows, axis, [(i, (i + s) % count) for i in range(count)])  8.48 us
    eq x16, other arithmetic, block_scores(): same = query_images[:, None] == images_blocked[kblock][None, :]  7.35 us
  transfers between devices with their start and end apart: 10, of which 5 were waited for; matrix products, arithmetic and copies ran while one was open for 28% of the time, Pallas kernels for 0%

profile of v1, /device:TPU:1, one launch (start us, length us, event | category | flops | bytes accessed | tf_op | source)
XLA Modules:
  0.0 246.0 jit_solution(18211003704983006111)
XLA Ops:
  6.5 1.8 pad_maximum_fusion.2
  8.4 1.3 convert_reduce_fusion.1
  9.6 1.4 fusion.124
  11.0 2.2 fusion.126
  13.2 2.1 collective-permute-start
  15.4 2.6 %collective-permute-start.1 = (bf16[256,1280]{1,0:T(8,128)(2,1)}, bf16[256,1280]{1,0:T(8,128)(2,1)}, u32[]{:S(2)}, u32[]{:S(2)}) collective-permute-start(bf16[256,1280]{1,0:T(8,128)(2,1)} %fusion.126), channel_id=1, source_target_pairs={{0,2},{1,3},{2,0},{3,1},{4,6},{5,7},{6,4},{7,5},{8,10},{9,11},{10,... | collective-permute-start | bytes 1966088 | tf_op jit(solution)/shard_map/ppermute | solution.py:33
  18.0 1.1 collective-permute-start.2
  19.0 1.4 fusion.189
  20.4 4.0 %fusion.148 = (s32[]{:T(128)}, s32[]{:T(128)}, s32[]{:T(128)}, s32[]{:T(128)}) fusion(s32[1,1024]{1,0:T(1,128)} %param.19, s32[]{:T(128)} %bitcast.17, s32[]{:T(128)} %bitcast.31, s32[]{:T(128)} %bitcast.16, s32[]{:T(128)} %bitcast.32), kind=kLoop, calls=%fused_computation.192 | loop fusion | flops 12284 | bytes 4128 | tf_op jit(solution)/shard_map/reduce_sum | solution.py:71
  31.2 1.3 fusion.188
  32.5 1.4 fusion.198
  33.8 14.8 %collective-permute-done.1 = bf16[256,1280]{1,0:T(8,128)(2,1)} collective-permute-done((bf16[256,1280]{1,0:T(8,128)(2,1)}, bf16[256,1280]{1,0:T(8,128)(2,1)}, u32[]{:S(2)}, u32[]{:S(2)}) %collective-permute-start.1) | collective-permute-done | bytes 655392 | tf_op jit(solution)/shard_map/ppermute | solution.py:33
  48.7 1.6 pad_maximum_fusion
  50.5 2.7 %fusion.114 = bf16[1024,960]{0,1:T(8,128)(2,1)S(1)} fusion(bf16[1280,960]{0,1:T(8,128)(2,1)S(1)} %bitcast.189, bf16[256,1280]{1,0:T(8,128)(2,1)S(1)} %get-tuple-element.331, bf16[256,1280]{1,0:T(8,128)(2,1)S(1)} %get-tuple-element.332, bf16[256,1280]{1,0:T(8,128)(2,1)S(1)} %get-tuple-element.333, bf16[256,1280]{1,0:T(8,128)(2,1)S(1)} %get-tuple-element.330), kind=kOutput, calls=%fused_computation.148 | convolution fusion | flops 2528051200 | bytes 7045120 | tf_op jit(solution)/shard_map/dot_general | solution.py:118
  53.5 1.0 copy-done.3
  55.4 0.9 copy.12
  56.4 1.1 fusion.187
  57.8 8.5 %while.44 = (s32[]{:T(128)}, f32[4,512]{1,0:T(4,128)S(1)}, f32[4,512]{1,0:T(4,128)S(1)}, s32[]{:T(128)}, s32[512]{0:T(512)}, /*index=5*/s32[8,128]{1,0:T(8,128)}...) while((s32[]{:T(128)}, f32[4,512]{1,0:T(4,128)S(1)}, ...), condition=%wide.region_7.8_spmd, body=%wide.region_4.7_spmd.sunk | while | flops 43323396 | bytes 2748055 | solution.py:96
  66.4 13.9 %while.45 = (s32[]{:T(128)}, f32[512,4,80]{0,2,1:T(8,128)S(1)}, s32[]{:T(128)}, bf16[8,128,4,80]{1,3,2,0:T(8,128)(2,1)}, s32[512]{0:T(512)}, /*index=5*/s32[8,12...) while((s32[]{:T(128)}, f32[512,4,80]{0,2,1:T(8,128)S(1)}, ...), condition=%wide.region_9.10_spmd, body=%wide.region_8.9_spmd.sunk | while | flops 85426176 | bytes 2117291 | solution.py:105
  67.2 0.8 broadcast_compare_fusion.9
  68.0 1.9 fusion.219
  70.6 0.8 broadcast_compare_fusion.9
  71.5 1.9 fusion.219
  74.1 0.8 broadcast_compare_fusion.9
  75.0 1.9 fusion.219
  77.6 0.8 broadcast_compare_fusion.9
  78.5 1.9 fusion.219
  81.4 5.8 %while.46 = (s32[]{:T(128)}, f32[4,512]{1,0:T(4,128)S(1)}, f32[4,512]{1,0:T(4,128)S(1)}, s32[]{:T(128)}, s32[512]{0:T(512)S(1)}, /*index=5*/s32[8,128]{1,0:T(8,1...) while((s32[]{:T(128)}, f32[4,512]{1,0:T(4,128)S(1)}, ...), condition=%wide.region_15.16_spmd, body=%wide.region_12.15_spmd.sunk | while | flops 43323396 | bytes 2748055 | solution.py:96
  87.3 11.3 %while.47 = (s32[]{:T(128)}, f32[512,4,80]{0,2,1:T(8,128)S(1)}, s32[]{:T(128)}, bf16[8,128,4,80]{1,3,2,0:T(8,128)(2,1)}, s32[512]{0:T(512)S(1)}, /*index=5*/s32[...) while((s32[]{:T(128)}, f32[512,4,80]{0,2,1:T(8,128)S(1)}, ...), condition=%wide.region_17.18_spmd, body=%wide.region_16.17_spmd.sunk | while | flops 85426176 | bytes 2117291 | solution.py:105
  88.3 1.9 fusion.226
  91.1 1.9 fusion.226
  93.9 1.9 fusion.226
  96.7 1.9 fusion.226
  98.7 2.9 %convolution_convert_fusion = bf16[1024,1280]{1,0:T(8,128)(2,1)S(1)} fusion(bf16[320,1280]{1,0:T(8,128)(2,1)} %param.22, bf16[512,320]{0,1:T(8,128)(2,1)S(1)} %bitcast.205, bf16[512,320]{0,1:T(8,128)(2,1)} %bitcast.204), kind=kOutput, calls=%fused_computation.93 | convolution fusion | flops 841482240 | bytes 4096000 | tf_op jit(solution)/shard_map/dot_general | solution.py:154
  101.6 1.4 dynamic-slice_bitcast_fusion.10
  102.9 1.1 collective-permute-start.3
  104.1 2.8 %collective-permute-start.4 = (bf16[256,1280]{1,0:T(8,128)(2,1)}, bf16[256,1280]{1,0:T(8,128)(2,1)}, u32[]{:S(2)}, u32[]{:S(2)}) collective-permute-start(bf16[256,1280]{1,0:T(8,128)(2,1)} %get-tuple-element.329), channel_id=1, source_target_pairs={{0,2},{1,3},{2,0},{3,1},{4,6},{5,7},{6,4},{7,5},{8,10},{9,11},{10,... | collective-permute-start | bytes 1966088 | tf_op jit(solution)/shard_map/ppermute | solution.py:51
  107.0 25.9 %collective-permute-done.3 = bf16[256,1280]{1,0:T(8,128)(2,1)} collective-permute-done((bf16[256,1280]{1,0:T(8,128)(2,1)}, bf16[256,1280]{1,0:T(8,128)(2,1)}, u32[]{:S(2)}, u32[]{:S(2)}) %collective-permute-start.3) | collective-permute-done | bytes 655392 | tf_op jit(solution)/shard_map/ppermute | solution.py:51
  132.9 14.6 %collective-permute-done.4 = bf16[256,1280]{1,0:T(8,128)(2,1)} collective-permute-done((bf16[256,1280]{1,0:T(8,128)(2,1)}, bf16[256,1280]{1,0:T(8,128)(2,1)}, u32[]{:S(2)}, u32[]{:S(2)}) %collective-permute-start.4) | collective-permute-done | bytes 655392 | tf_op jit(solution)/shard_map/ppermute | solution.py:51
  147.5 2.8 %convert_reduce_fusion = (f32[256]{0:T(256)S(1)}, bf16[256,1280]{1,0:T(8,128)(2,1)}) fusion(bf16[256,1280]{1,0:T(8,128)(2,1)} %collective-permute-done.5, bf16[256,1280]{1,0:T(8,128)(2,1)} %collective-permute-done.4, bf16[256,1280]{1,0:T(8,128)(2,1)} %collective-permute-done.3, bf16[4,256,1280]{2,1,0:T(8,128)(2,1)S(1)} %bitcast.197, s32[]{:T(128)S(6)} %select_n.125, ...), kind=kLoop, calls=%fused_computation.144 | loop fusion | flops 3931904 | bytes 3933188 | tf_op jit(solution)/shard_map/reduce_sum | solution.py:13
  150.3 1.4 fusion.121
  151.7 25.7 %fusion.190 = (f32[256]{0:T(256)S(1)}, f32[256,1280]{1,0:T(8,128)S(1)}) fusion(bf16[2,1280,5120]{1,2,0:T(8,128)(2,1)} %all-gather.2.cloned.1.call-done, bf16[256,1280]{1,0:T(8,128)(2,1)} %get-tuple-element.318, f32[1280]{0:T(1024)S(1)} %copy-done.6, f32[256]{0:T(256)S(1)} %add_rsqrt_fusion.1, f32[256]{0:T(256)S(1)} %broadcast_multiply_fusion.1), kind=kOutput, calls=%fused_computation.239 | convolution fusion | flops 6798704640 | bytes 28844032 | tf_op jit(solution)/shard_map/dot_general | solution.py:24
  178.0 1.2 reshape.214
  180.0 2.0 collective-permute-start.8
  182.3 28.0 %collective-permute-done.6 = bf16[64,5120]{1,0:T(8,128)(2,1)S(1)} collective-permute-done((bf16[64,5120]{1,0:T(8,128)(2,1)}, bf16[64,5120]{1,0:T(8,128)(2,1)S(1)}, u32[]{:S(2)}, u32[]{:S(2)}) %collective-permute-start.6) | collective-permute-done | bytes 655392 | tf_op jit(solution)/shard_map/ppermute | solution.py:33
  211.3 7.1 %fusion.133 = bf16[32,8,1024]{2,1,0:T(8,128)(2,1)S(1)} fusion(bf16[5120,1024]{1,0:T(8,128)(2,1)} %param.27, bf16[64,5120]{1,0:T(8,128)(2,1)S(1)} %get-tuple-element.324, bf16[64,5120]{1,0:T(8,128)(2,1)S(1)} %get-tuple-element.325, bf16[64,5120]{1,0:T(8,128)(2,1)S(1)} %get-tuple-element.326, bf16[64,5120]{1,0:T(8,128)(2,1)S(1)} %get-tuple-element.323), kind=kOutput, calls=%fused_computation.166 | convolution fusion | flops 2695102464 | bytes 13631488 | tf_op jit(solution)/shard_map/dot_general | solution.py:163
  218.3 20.0 %all_to_all.12 = bf16[32,8,1024]{2,1,0:T(8,128)(2,1)S(1)} all-to-all(bf16[32,8,1024]{2,1,0:T(8,128)(2,1)S(1)} %fusion.133), channel_id=1, replica_groups=mesh['zx'=16,'core'=2,'tok'=4] {'zx','core'}, dimensions={0} | all-to-all | bytes 1048576 | tf_op jit(solution)/shard_map/all_to_all | solution.py:168
  238.3 0.8 copy.76
  (127 shorter events, 26.1 us)
Async XLA Ops:
  6.5 43.9 %copy-start = (bf16[1280,3,320]{0,2,1:T(8,128)(2,1)S(1)}, bf16[1280,3,320]{0,2,1:T(8,128)(2,1)}, u32[]{:S(2)}) copy-start(bf16[1280,3,320]{0,2,1:T(8,128)(2,1)} %param.21) | copy-start | bytes 7372804
  6.5 145.2 %all-gather.2.cloned.1.call-start = ((), (), s32[]{:S(2)}) async-start(), calls=%async_computation.1 | async-start | bytes 26419200 | tf_op jit(solution)/shard_map/all_gather | solution.py:112
  13.2 20.6 %collective-permute-start = (bf16[256,1280]{1,0:T(8,128)(2,1)}, bf16[256,1280]{1,0:T(8,128)(2,1)S(1)}, u32[]{:S(2)}, u32[]{:S(2)}) collective-permute-start(bf16[256,1280]{1,0:T(8,128)(2,1)} %fusion.126), channel_id=1, source_target_pairs={{0,1},{1,2},{2,3},{3,0},{4,5},{5,6},{6,7},{7,4},{8,9},{9,10},{10,1... | collective-permute-start | bytes 1966088 | tf_op jit(solution)/shard_map/ppermute | solution.py:33
  15.4 33.3 %collective-permute-start.1 = (bf16[256,1280]{1,0:T(8,128)(2,1)}, bf16[256,1280]{1,0:T(8,128)(2,1)}, u32[]{:S(2)}, u32[]{:S(2)}) collective-permute-start(bf16[256,1280]{1,0:T(8,128)(2,1)} %fusion.126), channel_id=1, source_target_pairs={{0,2},{1,3},{2,0},{3,1},{4,6},{5,7},{6,4},{7,5},{8,10},{9,11},{10,... | collective-permute-start | bytes 1966088 | tf_op jit(solution)/shard_map/ppermute | solution.py:33
  18.0 30.7 %collective-permute-start.2 = (bf16[256,1280]{1,0:T(8,128)(2,1)}, bf16[256,1280]{1,0:T(8,128)(2,1)}, u32[]{:S(2)}, u32[]{:S(2)}) collective-permute-start(bf16[256,1280]{1,0:T(8,128)(2,1)} %fusion.126), channel_id=1, source_target_pairs={{0,3},{1,0},{2,1},{3,2},{4,7},{5,4},{6,5},{7,6},{8,11},{9,8},{10,9... | collective-permute-start | bytes 1966088 | tf_op jit(solution)/shard_map/ppermute | solution.py:33
  53.2 1.3 copy-start.3
  66.4 15.0 %copy-start.4 = (s32[1,512]{1,0:T(1,128)S(1)}, s32[1,512]{1,0:T(1,128)}, u32[]{:S(2)}) copy-start(s32[1,512]{1,0:T(1,128)} %get-tuple-element.339) | copy-start | bytes 6148
  98.7 48.8 %copy-start.2 = (bf16[256,1280]{1,0:T(8,128)(2,1)S(1)}, bf16[256,1280]{1,0:T(8,128)(2,1)}, u32[]{:S(2)}) copy-start(bf16[256,1280]{1,0:T(8,128)(2,1)} %param.18) | copy-start | bytes 1966084
  101.5 50.2 %copy-start.6 = (f32[1280]{0:T(1024)S(1)}, f32[1280]{0:T(1024)}, u32[]{:S(2)}) copy-start(f32[1280]{0:T(1024)} %param.23) | copy-start | bytes 15364
  102.9 29.9 %collective-permute-start.3 = (bf16[256,1280]{1,0:T(8,128)(2,1)}, bf16[256,1280]{1,0:T(8,128)(2,1)}, u32[]{:S(2)}, u32[]{:S(2)}) collective-permute-start(bf16[256,1280]{1,0:T(8,128)(2,1)} %get-tuple-element.327), channel_id=1, source_target_pairs={{0,1},{1,2},{2,3},{3,0},{4,5},{5,6},{6,7},{7,4},{8,9},{9,10},{10,1... | collective-permute-start | bytes 1966088 | tf_op jit(solution)/shard_map/ppermute | solution.py:51
  104.1 43.4 %collective-permute-start.4 = (bf16[256,1280]{1,0:T(8,128)(2,1)}, bf16[256,1280]{1,0:T(8,128)(2,1)}, u32[]{:S(2)}, u32[]{:S(2)}) collective-permute-start(bf16[256,1280]{1,0:T(8,128)(2,1)} %get-tuple-element.329), channel_id=1, source_target_pairs={{0,2},{1,3},{2,0},{3,1},{4,6},{5,7},{6,4},{7,5},{8,10},{9,11},{10,... | collective-permute-start | bytes 1966088 | tf_op jit(solution)/shard_map/ppermute | solution.py:51
  106.9 40.6 %collective-permute-start.5 = (bf16[256,1280]{1,0:T(8,128)(2,1)}, bf16[256,1280]{1,0:T(8,128)(2,1)}, u32[]{:S(2)}, u32[]{:S(2)}) collective-permute-start(bf16[256,1280]{1,0:T(8,128)(2,1)} %get-tuple-element.328), channel_id=1, source_target_pairs={{0,3},{1,0},{2,1},{3,2},{4,7},{5,4},{6,5},{7,6},{8,11},{9,8},{10,9... | collective-permute-start | bytes 1966088 | tf_op jit(solution)/shard_map/ppermute | solution.py:51
  151.7 26.1 %copy-start.5 = (f32[1280]{0:T(1024)S(1)}, f32[1280]{0:T(1024)}, u32[]{:S(2)}) copy-start(f32[1280]{0:T(1024)} %param.26) | copy-start | bytes 15364
  179.3 31.1 %collective-permute-start.6 = (bf16[64,5120]{1,0:T(8,128)(2,1)}, bf16[64,5120]{1,0:T(8,128)(2,1)S(1)}, u32[]{:S(2)}, u32[]{:S(2)}) collective-permute-start(bf16[64,5120]{1,0:T(8,128)(2,1)} %reshape.214), channel_id=1, source_target_pairs={{0,1},{1,2},{2,3},{3,0},{4,5},{5,6},{6,7},{7,4},{8,9},{9,10},{10,1... | collective-permute-start | bytes 1966088 | tf_op jit(solution)/shard_map/ppermute | solution.py:33
  179.3 31.1 %collective-permute-start.7 = (bf16[64,5120]{1,0:T(8,128)(2,1)}, bf16[64,5120]{1,0:T(8,128)(2,1)S(1)}, u32[]{:S(2)}, u32[]{:S(2)}) collective-permute-start(bf16[64,5120]{1,0:T(8,128)(2,1)} %reshape.214), channel_id=1, source_target_pairs={{0,2},{1,3},{2,0},{3,1},{4,6},{5,7},{6,4},{7,5},{8,10},{9,11},{10,... | collective-permute-start | bytes 1966088 | tf_op jit(solution)/shard_map/ppermute | solution.py:33
  180.0 30.8 %collective-permute-start.8 = (bf16[64,5120]{1,0:T(8,128)(2,1)}, bf16[64,5120]{1,0:T(8,128)(2,1)S(1)}, u32[]{:S(2)}, u32[]{:S(2)}) collective-permute-start(bf16[64,5120]{1,0:T(8,128)(2,1)} %reshape.214), channel_id=1, source_target_pairs={{0,3},{1,0},{2,1},{3,2},{4,7},{5,4},{6,5},{7,6},{8,11},{9,8},{10,9... | collective-permute-start | bytes 1966088 | tf_op jit(solution)/shard_map/ppermute | solution.py:33
  211.3 27.9 %copy-start.1 = (bf16[1280,3,320]{0,2,1:T(8,128)(2,1)S(1)}, bf16[1280,3,320]{0,2,1:T(8,128)(2,1)}, u32[]{:S(2)}) copy-start(bf16[1280,3,320]{0,2,1:T(8,128)(2,1)} %param.21) | copy-start | bytes 7372804
Sparse Core Ops, SparseCore 0:
  10.3 126.5 all-gather.1

commit v2 on v1

--- a/solution.py
+++ b/solution.py
@@ -165,7 +165,11 @@
         w_proj,
         preferred_element_type=jnp.float32,
     ).astype(jnp.bfloat16)
-    return lax.all_to_all(projected, ("zx", "core"), split_axis=0, concat_axis=0, tiled=True)
+    zx, core = lax.axis_size("zx"), lax.axis_size("core")
+    blocks = projected.reshape(zx, core, projected.shape[0] // (zx * core), projected.shape[1])
+    blocks = lax.all_to_all(blocks, "core", split_axis=1, concat_axis=1, tiled=True)
+    blocks = lax.all_to_all(blocks, "zx", split_axis=0, concat_axis=0, tiled=True)
+    return blocks.reshape(projected.shape)
 
 
 def solution(mesh):

time: 248 us -> 241 us (0.972)
  waiting for transfers between devices: 83.7 us -> 104 us
  local copies, waits for them, and re-layouts: 23.5 us -> 7.23 us
  matrix products: 56.5 us -> 47.1 us
  other arithmetic: 28.4 us -> 22.8 us
  blocking collectives: 20 us -> 23 us
    all_gather x1, waiting for transfers between devices: 0.02 us -> 12.6 us  [layer(): lax.all_gather(jnp.stack([w_up, w_down_t]), ('zx', 'core', 'tok'), axis=2...]
    dynamic_slice x16, local copies, waits for them, and re-layouts: 11.2 us -> 0.12 us  [block_scores(): same = query_images[:, None] == images_blocked[kblock][None, :]]
    dot_general x8, matrix products: 14.9 us -> 5.59 us  [add_values(): jnp.einsum('hqk,khd->qhd', weights, values_blocked[kblock], preferred_ele...]
    ppermute x3, waiting for transfers between devices: 40.5 us -> 48.4 us  [permute_scatter(): lax.ppermute(outgoing, axis, [(i, (i + s) % count) for i in range(count)])]
    eq x16, other arithmetic: 7.35 us -> 1.67 us  [block_scores(): same = query_images[:, None] == images_blocked[kblock][None, :]]
    all_to_all x1 -> x2, blocking collectives: 20 us -> 23 us  [the longest x1 18.1 us: layer(): lax.all_to_all(blocks, 'zx', split_axis=0, concat_axis=0, tiled=True)]
  transfers between devices with their start and end apart: 10 -> 10, of which waited for: 5 -> 6; matrix products, arithmetic and copies ran while one was open for 28% -> 16% of each run, Pallas kernels for 0% -> 0%
where the time goes in v2:
time: 241 us; the launch traced here: 240 us
  waiting for transfers between devices  104 us (43%)
  matrix products  47.1 us (20%)
  blocking collectives  23 us (10%)
  other arithmetic  22.8 us (9%)
  between operations  20.5 us (9%)
  starting transfers between devices  14 us (6%)
  local copies, waits for them, and re-layouts  7.23 us (3%)
    ppermute x3, waiting for transfers between devices, permute_scatter(): lax.ppermute(outgoing, axis, [(i, (i + s) % count) for i in range(count)])  48.4 us
    ppermute x6, waiting for transfers between devices, permute_gather(): lax.ppermute(rows, axis, [(i, (i + s) % count) for i in range(count)])  43.3 us
    dot_general x1, matrix products, hidden_fold(): lax.dot_general(hidden, down_piece, (((1,), (1,)), ((), ())), preferred_e...  25.7 us
    all_to_all x1, blocking collectives, layer(): lax.all_to_all(blocks, 'zx', split_axis=0, concat_axis=0, tiled=True)  18.1 us
    all_gather x1, waiting for transfers between devices, layer(): lax.all_gather(jnp.stack([w_up, w_down_t]), ('zx', 'core', 'tok'), axis=2...  12.6 us
    ppermute x6, starting transfers between devices, permute_gather(): lax.ppermute(rows, axis, [(i, (i + s) % count) for i in range(count)])  9.85 us
    dot_general x1, matrix products, layer(): jnp.dot(permute_gather(merged, 'tok'), w_proj, preferred_element_type=jnp...  7.06 us
    dot_general x8, matrix products, add_values(): jnp.einsum('hqk,khd->qhd', weights, values_blocked[kblock], preferred_ele...  5.59 us
  transfers between devices with their start and end apart: 10, of which 6 were waited for; matrix products, arithmetic and copies ran while one was open for 16% of the time, Pallas kernels for 0%

profile of v2, /device:TPU:1, one launch (start us, length us, event | category | flops | bytes accessed | tf_op | source)
XLA Modules:
  0.0 239.9 jit_solution(15140468384713812009)
XLA Ops:
  6.5 1.8 pad_maximum_fusion.2
  8.4 1.3 convert_reduce_fusion.1
  9.6 1.4 fusion.126
  11.0 2.2 fusion.128
  13.2 2.1 collective-permute-start
  15.4 2.6 %collective-permute-start.1 = (bf16[256,1280]{1,0:T(8,128)(2,1)}, bf16[256,1280]{1,0:T(8,128)(2,1)}, u32[]{:S(2)}, u32[]{:S(2)}) collective-permute-start(bf16[256,1280]{1,0:T(8,128)(2,1)} %fusion.128), channel_id=1, source_target_pairs={{0,2},{1,3},{2,0},{3,1},{4,6},{5,7},{6,4},{7,5},{8,10},{9,11},{10,... | collective-permute-start | bytes 1966088 | tf_op jit(solution)/shard_map/ppermute | solution.py:33
  18.0 1.1 collective-permute-start.2
  19.0 1.4 fusion.188
  20.4 4.0 %fusion.147 = (s32[]{:T(128)}, s32[]{:T(128)}, s32[]{:T(128)}, s32[]{:T(128)}) fusion(s32[1,1024]{1,0:T(1,128)} %param.19, s32[]{:T(128)} %bitcast.17, s32[]{:T(128)} %bitcast.31, s32[]{:T(128)} %bitcast.16, s32[]{:T(128)} %bitcast.32), kind=kLoop, calls=%fused_computation.189 | loop fusion | flops 12284 | bytes 4128 | tf_op jit(solution)/shard_map/reduce_sum | solution.py:71
  31.2 0.7 fusion.187
  31.9 1.4 fusion.199
  33.3 15.4 %collective-permute-done.1 = bf16[256,1280]{1,0:T(8,128)(2,1)} collective-permute-done((bf16[256,1280]{1,0:T(8,128)(2,1)}, bf16[256,1280]{1,0:T(8,128)(2,1)}, u32[]{:S(2)}, u32[]{:S(2)}) %collective-permute-start.1) | collective-permute-done | bytes 655392 | tf_op jit(solution)/shard_map/ppermute | solution.py:33
  48.7 1.6 pad_maximum_fusion
  50.5 2.7 %fusion.116 = bf16[1024,960]{0,1:T(8,128)(2,1)S(1)} fusion(bf16[1280,960]{0,1:T(8,128)(2,1)S(1)} %bitcast.198, bf16[256,1280]{1,0:T(8,128)(2,1)S(1)} %get-tuple-element.403, bf16[256,1280]{1,0:T(8,128)(2,1)S(1)} %get-tuple-element.404, bf16[256,1280]{1,0:T(8,128)(2,1)S(1)} %get-tuple-element.405, bf16[256,1280]{1,0:T(8,128)(2,1)S(1)} %get-tuple-element.402), kind=kOutput, calls=%fused_computation.146 | convolution fusion | flops 2528051200 | bytes 7045120 | tf_op jit(solution)/shard_map/dot_general | solution.py:118
  53.9 3.0 %while.44 = (s32[]{:T(128)}, f32[4,512]{1,0:T(4,128)S(1)}, f32[4,512]{1,0:T(4,128)S(1)}, s32[]{:T(128)}, s32[512]{0:T(512)S(1)}, /*index=5*/s32[8,128]{1,0:T(8,1...) while((s32[]{:T(128)}, f32[4,512]{1,0:T(4,128)S(1)}, ...), condition=%wide.region_7.8_spmd, body=%wide.region_4.7_spmd.sunk | while | flops 43323396 | bytes 2748055 | solution.py:96
  57.0 3.4 %while.45 = (s32[]{:T(128)}, f32[512,4,80]{0,2,1:T(8,128)S(1)}, s32[]{:T(128)}, bf16[8,128,4,80]{1,3,2,0:T(8,128)(2,1)S(1)}, s32[512]{0:T(512)S(1)}, /*index=5*/...) while((s32[]{:T(128)}, f32[512,4,80]{0,2,1:T(8,128)S(1)}, ...), condition=%wide.region_9.10_spmd, body=%wide.region_8.9_spmd.sunk | while | flops 85426176 | bytes 1954467 | solution.py:105
  57.2 0.7 fusion.220
  58.0 0.7 fusion.220
  58.9 0.7 fusion.220
  59.8 0.7 fusion.220
  60.5 0.8 convert_element_type.85
  61.2 3.0 %while.46 = (s32[]{:T(128)}, f32[4,512]{1,0:T(4,128)S(1)}, f32[4,512]{1,0:T(4,128)S(1)}, s32[]{:T(128)}, s32[512]{0:T(512)S(1)}, /*index=5*/s32[8,128]{1,0:T(8,1...) while((s32[]{:T(128)}, f32[4,512]{1,0:T(4,128)S(1)}, ...), condition=%wide.region_15.16_spmd, body=%wide.region_12.15_spmd.sunk | while | flops 43323396 | bytes 2748055 | solution.py:96
  61.4 0.4 fusion.222
  64.4 3.4 %while.47 = (s32[]{:T(128)}, f32[512,4,80]{0,2,1:T(8,128)S(1)}, s32[]{:T(128)}, bf16[8,128,4,80]{1,3,2,0:T(8,128)(2,1)S(1)}, s32[512]{0:T(512)S(1)}, /*index=5*/...) while((s32[]{:T(128)}, f32[512,4,80]{0,2,1:T(8,128)S(1)}, ...), condition=%wide.region_17.18_spmd, body=%wide.region_16.17_spmd.sunk | while | flops 85426176 | bytes 1954467 | solution.py:105
  64.5 0.7 fusion.227
  65.4 0.7 fusion.227
  66.2 0.7 fusion.227
  67.1 0.7 fusion.227
  67.9 2.9 %convolution_convert_fusion = bf16[1024,1280]{1,0:T(8,128)(2,1)S(1)} fusion(bf16[320,1280]{1,0:T(8,128)(2,1)} %param.22, bf16[512,320]{0,1:T(8,128)(2,1)S(1)} %bitcast.212, bf16[512,320]{0,1:T(8,128)(2,1)} %bitcast.211), kind=kOutput, calls=%fused_computation.91 | convolution fusion | flops 841482240 | bytes 4096000 | tf_op jit(solution)/shard_map/dot_general | solution.py:154
  70.8 1.4 dynamic-slice_bitcast_fusion.8
  72.2 1.1 collective-permute-start.3
  73.3 2.9 %collective-permute-start.4 = (bf16[256,1280]{1,0:T(8,128)(2,1)}, bf16[256,1280]{1,0:T(8,128)(2,1)}, u32[]{:S(2)}, u32[]{:S(2)}) collective-permute-start(bf16[256,1280]{1,0:T(8,128)(2,1)} %get-tuple-element.401), channel_id=1, source_target_pairs={{0,2},{1,3},{2,0},{3,1},{4,6},{5,7},{6,4},{7,5},{8,10},{9,11},{10,... | collective-permute-start | bytes 1966088 | tf_op jit(solution)/shard_map/ppermute | solution.py:51
  76.3 16.4 %collective-permute-done.3 = bf16[256,1280]{1,0:T(8,128)(2,1)} collective-permute-done((bf16[256,1280]{1,0:T(8,128)(2,1)}, bf16[256,1280]{1,0:T(8,128)(2,1)}, u32[]{:S(2)}, u32[]{:S(2)}) %collective-permute-start.3) | collective-permute-done | bytes 655392 | tf_op jit(solution)/shard_map/ppermute | solution.py:51
  92.7 32.0 %collective-permute-done.4 = bf16[256,1280]{1,0:T(8,128)(2,1)} collective-permute-done((bf16[256,1280]{1,0:T(8,128)(2,1)}, bf16[256,1280]{1,0:T(8,128)(2,1)}, u32[]{:S(2)}, u32[]{:S(2)}) %collective-permute-start.4) | collective-permute-done | bytes 655392 | tf_op jit(solution)/shard_map/ppermute | solution.py:51
  124.7 2.9 %convert_reduce_fusion = (f32[256]{0:T(256)S(1)}, bf16[256,1280]{1,0:T(8,128)(2,1)}) fusion(bf16[256,1280]{1,0:T(8,128)(2,1)} %collective-permute-done.5, bf16[256,1280]{1,0:T(8,128)(2,1)} %collective-permute-done.4, bf16[256,1280]{1,0:T(8,128)(2,1)} %collective-permute-done.3, bf16[4,256,1280]{2,1,0:T(8,128)(2,1)S(1)} %bitcast.202, s32[]{:T(128)S(6)} %select_n.125, ...), kind=kLoop, calls=%fused_computation.142 | loop fusion | flops 3931904 | bytes 3933188 | tf_op jit(solution)/shard_map/reduce_sum | solution.py:13
  127.6 1.4 fusion.123
  129.1 12.6 %all-gather.2.cloned.1.call-done = bf16[2,1280,5120]{1,2,0:T(8,128)(2,1)} async-done(((bf16[2,1280,40]{1,2,0:T(8,128)(2,1)}), bf16[2,1280,5120]{1,2,0:T(8,128)(2,1)}) %all-gather.2.cloned.1.call-update) | async-done | bytes 26214416 | tf_op jit(solution)/shard_map/all_gather | solution.py:112
  141.7 25.7 %fusion.189 = (f32[256]{0:T(256)S(1)}, f32[256,1280]{1,0:T(8,128)S(1)}) fusion(bf16[2,1280,5120]{1,2,0:T(8,128)(2,1)} %all-gather.2.cloned.1.call-done, bf16[256,1280]{1,0:T(8,128)(2,1)} %get-tuple-element.390, f32[1280]{0:T(1024)S(1)} %copy-done.5, f32[256]{0:T(256)S(1)} %add_rsqrt_fusion.1, f32[256]{0:T(256)S(1)} %broadcast_multiply_fusion.1), kind=kOutput, calls=%fused_computation.236 | convolution fusion | flops 6798704640 | bytes 28844032 | tf_op jit(solution)/shard_map/dot_general | solution.py:24
  168.0 1.2 reshape.218
  169.2 1.3 collective-permute-start.6
  170.6 2.2 collective-permute-start.7
  172.8 0.5 collective-permute-start.8
  173.7 13.0 %collective-permute-done.6 = bf16[64,5120]{1,0:T(8,128)(2,1)S(1)} collective-permute-done((bf16[64,5120]{1,0:T(8,128)(2,1)}, bf16[64,5120]{1,0:T(8,128)(2,1)S(1)}, u32[]{:S(2)}, u32[]{:S(2)}) %collective-permute-start.6) | collective-permute-done | bytes 655392 | tf_op jit(solution)/shard_map/ppermute | solution.py:33
  186.7 14.9 %collective-permute-done.7 = bf16[64,5120]{1,0:T(8,128)(2,1)S(1)} collective-permute-done((bf16[64,5120]{1,0:T(8,128)(2,1)}, bf16[64,5120]{1,0:T(8,128)(2,1)S(1)}, u32[]{:S(2)}, u32[]{:S(2)}) %collective-permute-start.7) | collective-permute-done | bytes 655392 | tf_op jit(solution)/shard_map/ppermute | solution.py:33
  202.1 7.1 %fusion.132 = bf16[256,1024]{1,0:T(8,128)(2,1)S(1)} fusion(bf16[5120,1024]{1,0:T(8,128)(2,1)} %param.27, bf16[64,5120]{1,0:T(8,128)(2,1)S(1)} %get-tuple-element.396, bf16[64,5120]{1,0:T(8,128)(2,1)S(1)} %get-tuple-element.397, bf16[64,5120]{1,0:T(8,128)(2,1)S(1)} %get-tuple-element.398, bf16[64,5120]{1,0:T(8,128)(2,1)S(1)} %get-tuple-element.395), kind=kOutput, calls=%fused_computation.163 | convolution fusion | flops 2695102464 | bytes 13631488 | tf_op jit(solution)/shard_map/dot_general | solution.py:163
  209.2 4.9 %all_to_all.10 = bf16[16,2,8,1024]{3,2,0,1:T(8,128)(2,1)S(1)} all-to-all(bf16[16,2,8,1024]{3,2,0,1:T(8,128)(2,1)S(1)} %copy.36), channel_id=1, replica_groups=mesh['zx'=16,'core'=2,'tok'=4] {'core'}, dimensions={1} | all-to-all | bytes 1048576 | tf_op jit(solution)/shard_map/all_to_all | solution.py:170
  214.2 18.1 %all_to_all.11 = bf16[16,2,8,1024]{3,2,1,0:T(8,128)(2,1)S(1)} all-to-all(bf16[16,2,8,1024]{3,2,1,0:T(8,128)(2,1)S(1)} %copy.37), channel_id=1, replica_groups=mesh['zx'=16,'core'=2,'tok'=4] {'zx'}, dimensions={0} | all-to-all | bytes 1048576 | tf_op jit(solution)/shard_map/all_to_all | solution.py:171
  232.3 0.8 copy.73
  (117 shorter events, 8.9 us)
Async XLA Ops:
  6.5 43.9 %copy-start = (bf16[1280,3,320]{0,2,1:T(8,128)(2,1)S(1)}, bf16[1280,3,320]{0,2,1:T(8,128)(2,1)}, u32[]{:S(2)}) copy-start(bf16[1280,3,320]{0,2,1:T(8,128)(2,1)} %param.21) | copy-start | bytes 7372804
  6.5 135.2 %all-gather.2.cloned.1.call-start = ((), (), s32[]{:S(2)}) async-start(), calls=%async_computation.2 | async-start | bytes 26419200 | tf_op jit(solution)/shard_map/all_gather | solution.py:112
  13.2 20.0 %collective-permute-start = (bf16[256,1280]{1,0:T(8,128)(2,1)}, bf16[256,1280]{1,0:T(8,128)(2,1)S(1)}, u32[]{:S(2)}, u32[]{:S(2)}) collective-permute-start(bf16[256,1280]{1,0:T(8,128)(2,1)} %fusion.128), channel_id=1, source_target_pairs={{0,1},{1,2},{2,3},{3,0},{4,5},{5,6},{6,7},{7,4},{8,9},{9,10},{10,1... | collective-permute-start | bytes 1966088 | tf_op jit(solution)/shard_map/ppermute | solution.py:33
  15.4 33.3 %collective-permute-start.1 = (bf16[256,1280]{1,0:T(8,128)(2,1)}, bf16[256,1280]{1,0:T(8,128)(2,1)}, u32[]{:S(2)}, u32[]{:S(2)}) collective-permute-start(bf16[256,1280]{1,0:T(8,128)(2,1)} %fusion.128), channel_id=1, source_target_pairs={{0,2},{1,3},{2,0},{3,1},{4,6},{5,7},{6,4},{7,5},{8,10},{9,11},{10,... | collective-permute-start | bytes 1966088 | tf_op jit(solution)/shard_map/ppermute | solution.py:33
  18.0 30.7 %collective-permute-start.2 = (bf16[256,1280]{1,0:T(8,128)(2,1)}, bf16[256,1280]{1,0:T(8,128)(2,1)}, u32[]{:S(2)}, u32[]{:S(2)}) collective-permute-start(bf16[256,1280]{1,0:T(8,128)(2,1)} %fusion.128), channel_id=1, source_target_pairs={{0,3},{1,0},{2,1},{3,2},{4,7},{5,4},{6,5},{7,6},{8,11},{9,8},{10,9... | collective-permute-start | bytes 1966088 | tf_op jit(solution)/shard_map/ppermute | solution.py:33
  53.2 0.7 copy-start.3
  67.9 56.9 %copy-start.2 = (bf16[256,1280]{1,0:T(8,128)(2,1)S(1)}, bf16[256,1280]{1,0:T(8,128)(2,1)}, u32[]{:S(2)}) copy-start(bf16[256,1280]{1,0:T(8,128)(2,1)} %param.18) | copy-start | bytes 1966084
  70.8 71.0 %copy-start.5 = (f32[1280]{0:T(1024)S(1)}, f32[1280]{0:T(1024)}, u32[]{:S(2)}) copy-start(f32[1280]{0:T(1024)} %param.23) | copy-start | bytes 15364
  72.2 20.6 %collective-permute-start.3 = (bf16[256,1280]{1,0:T(8,128)(2,1)}, bf16[256,1280]{1,0:T(8,128)(2,1)}, u32[]{:S(2)}, u32[]{:S(2)}) collective-permute-start(bf16[256,1280]{1,0:T(8,128)(2,1)} %get-tuple-element.399), channel_id=1, source_target_pairs={{0,1},{1,2},{2,3},{3,0},{4,5},{5,6},{6,7},{7,4},{8,9},{9,10},{10,1... | collective-permute-start | bytes 1966088 | tf_op jit(solution)/shard_map/ppermute | solution.py:51
  73.3 51.5 %collective-permute-start.4 = (bf16[256,1280]{1,0:T(8,128)(2,1)}, bf16[256,1280]{1,0:T(8,128)(2,1)}, u32[]{:S(2)}, u32[]{:S(2)}) collective-permute-start(bf16[256,1280]{1,0:T(8,128)(2,1)} %get-tuple-element.401), channel_id=1, source_target_pairs={{0,2},{1,3},{2,0},{3,1},{4,6},{5,7},{6,4},{7,5},{8,10},{9,11},{10,... | collective-permute-start | bytes 1966088 | tf_op jit(solution)/shard_map/ppermute | solution.py:51
  76.2 48.6 %collective-permute-start.5 = (bf16[256,1280]{1,0:T(8,128)(2,1)}, bf16[256,1280]{1,0:T(8,128)(2,1)}, u32[]{:S(2)}, u32[]{:S(2)}) collective-permute-start(bf16[256,1280]{1,0:T(8,128)(2,1)} %get-tuple-element.400), channel_id=1, source_target_pairs={{0,3},{1,0},{2,1},{3,2},{4,7},{5,4},{6,5},{7,6},{8,11},{9,8},{10,9... | collective-permute-start | bytes 1966088 | tf_op jit(solution)/shard_map/ppermute | solution.py:51
  129.1 38.7 %copy-start.4 = (f32[1280]{0:T(1024)S(1)}, f32[1280]{0:T(1024)}, u32[]{:S(2)}) copy-start(f32[1280]{0:T(1024)} %param.26) | copy-start | bytes 15364
  169.2 17.4 %collective-permute-start.6 = (bf16[64,5120]{1,0:T(8,128)(2,1)}, bf16[64,5120]{1,0:T(8,128)(2,1)S(1)}, u32[]{:S(2)}, u32[]{:S(2)}) collective-permute-start(bf16[64,5120]{1,0:T(8,128)(2,1)} %reshape.218), channel_id=1, source_target_pairs={{0,1},{1,2},{2,3},{3,0},{4,5},{5,6},{6,7},{7,4},{8,9},{9,10},{10,1... | collective-permute-start | bytes 1966088 | tf_op jit(solution)/shard_map/ppermute | solution.py:33
  170.6 31.0 %collective-permute-start.7 = (bf16[64,5120]{1,0:T(8,128)(2,1)}, bf16[64,5120]{1,0:T(8,128)(2,1)S(1)}, u32[]{:S(2)}, u32[]{:S(2)}) collective-permute-start(bf16[64,5120]{1,0:T(8,128)(2,1)} %reshape.218), channel_id=1, source_target_pairs={{0,2},{1,3},{2,0},{3,1},{4,6},{5,7},{6,4},{7,5},{8,10},{9,11},{10,... | collective-permute-start | bytes 1966088 | tf_op jit(solution)/shard_map/ppermute | solution.py:33
  172.8 28.8 %collective-permute-start.8 = (bf16[64,5120]{1,0:T(8,128)(2,1)}, bf16[64,5120]{1,0:T(8,128)(2,1)S(1)}, u32[]{:S(2)}, u32[]{:S(2)}) collective-permute-start(bf16[64,5120]{1,0:T(8,128)(2,1)} %reshape.218), channel_id=1, source_target_pairs={{0,3},{1,0},{2,1},{3,2},{4,7},{5,4},{6,5},{7,6},{8,11},{9,8},{10,9... | collective-permute-start | bytes 1966088 | tf_op jit(solution)/shard_map/ppermute | solution.py:33
  202.1 31.0 %copy-start.1 = (bf16[1280,3,320]{0,2,1:T(8,128)(2,1)S(1)}, bf16[1280,3,320]{0,2,1:T(8,128)(2,1)}, u32[]{:S(2)}) copy-start(bf16[1280,3,320]{0,2,1:T(8,128)(2,1)} %param.21) | copy-start | bytes 7372804
Sparse Core Ops, SparseCore 0:
  10.3 131.3 all-gather.1

commit v3 on v1

--- a/solution.py
+++ b/solution.py
@@ -26,11 +26,11 @@
     )
 
 
-def permute_gather(rows, axis):
+def permute_gather(rows, axis, each=lambda rows: rows):
     count = lax.axis_size(axis)
     here = lax.axis_index(axis)
-    shifted = [rows] + [
-        lax.ppermute(rows, axis, [(i, (i + s) % count) for i in range(count)])
+    shifted = [each(rows)] + [
+        each(lax.ppermute(rows, axis, [(i, (i + s) % count) for i in range(count)]))
         for s in range(1, count)
     ]
     stacked = jnp.stack(shifted)
@@ -160,11 +160,11 @@
     second = first.astype(jnp.float32) + mlp_out
     normed_merge = layer_norm(second, gain_merge).astype(jnp.bfloat16)
     merged = normed_merge.reshape(inputs.shape[0] // 4, 4 * inputs.shape[1])
-    projected = jnp.dot(
-        permute_gather(merged, "tok"),
-        w_proj,
-        preferred_element_type=jnp.float32,
-    ).astype(jnp.bfloat16)
+    projected = permute_gather(
+        merged,
+        "tok",
+        lambda rows: jnp.dot(rows, w_proj, preferred_element_type=jnp.float32).astype(jnp.bfloat16),
+    )
     return lax.all_to_all(projected, ("zx", "core"), split_axis=0, concat_axis=0, tiled=True)
 
 

time: 248 us -> 242 us (0.976)
  local copies, waits for them, and re-layouts: 23.5 us -> 12.6 us
  waiting for transfers between devices: 83.7 us -> 92.2 us
  other arithmetic: 28.4 us -> 20 us
  matrix products: 56.5 us -> 62 us
    ppermute x3, waiting for transfers between devices: 40.5 us -> 54.5 us  [permute_scatter(): lax.ppermute(outgoing, axis, [(i, (i + s) % count) for i in range(count)])]
    dynamic_slice x16, local copies, waits for them, and re-layouts: 11.2 us -> 0.13 us  [block_scores(): same = query_images[:, None] == images_blocked[kblock][None, :]]
    dot_general x1 -> x4, matrix products: 7.06 us -> 15.9 us  [layer(): jnp.dot(rows, w_proj, preferred_element_type=jnp.float32)]
    ppermute x6, waiting for transfers between devices: 43.2 us -> 37.7 us  [permute_gather(): lax.ppermute(rows, axis, [(i, (i + s) % count) for i in range(count)])]
    eq x16, other arithmetic: 7.35 us -> 1.92 us  [block_scores(): same = query_images[:, None] == images_blocked[kblock][None, :]]
    dot_general x1, matrix products: 25.7 us -> 21.7 us  [hidden_fold(): lax.dot_general(hidden, down_piece, (((1,), (1,)), ((), ())), preferred_e...]
  transfers between devices with their start and end apart: 10 -> 10, of which waited for: 5 -> 4; matrix products, arithmetic and copies ran while one was open for 28% -> 27% of each run, Pallas kernels for 0% -> 0%
where the time goes in v3:
time: 242 us; the launch traced here: 241 us
  waiting for transfers between devices  92.2 us (38%)
  matrix products  62 us (26%)
  between operations  20.4 us (8%)
  other arithmetic  20 us (8%)
  blocking collectives  19.8 us (8%)
  starting transfers between devices  12.8 us (5%)
  local copies, waits for them, and re-layouts  12.6 us (5%)
    ppermute x3, waiting for transfers between devices, permute_scatter(): lax.ppermute(outgoing, axis, [(i, (i + s) % count) for i in range(count)])  54.5 us
    ppermute x6, waiting for transfers between devices, permute_gather(): lax.ppermute(rows, axis, [(i, (i + s) % count) for i in range(count)])  37.7 us
    dot_general x1, matrix products, hidden_fold(): lax.dot_general(hidden, down_piece, (((1,), (1,)), ((), ())), preferred_e...  21.7 us
    all_to_all x1, blocking collectives, layer(): lax.all_to_all(projected, ('zx', 'core'), split_axis=0, concat_axis=0, ti...  19.8 us
    dot_general x4, matrix products, layer(): jnp.dot(rows, w_proj, preferred_element_type=jnp.float32)  15.9 us
    dot_general x8, matrix products, add_values(): jnp.einsum('hqk,khd->qhd', weights, values_blocked[kblock], preferred_ele...  15.7 us
    ppermute x6, starting transfers between devices, permute_gather(): lax.ppermute(rows, axis, [(i, (i + s) % count) for i in range(count)])  8.54 us
  transfers between devices with their start and end apart: 10, of which 4 were waited for; matrix products, arithmetic and copies ran while one was open for 27% of the time, Pallas kernels for 0%

profile of v3, /device:TPU:1, one launch (start us, length us, event | category | flops | bytes accessed | tf_op | source)
XLA Modules:
  0.0 240.7 jit_solution(13048240974496488691)
XLA Ops:
  6.5 1.8 pad_maximum_fusion.2
  8.4 1.3 convert_reduce_fusion.1
  9.6 1.4 fusion.116
  11.0 2.2 fusion.118
  13.3 2.1 collective-permute-start
  15.4 2.6 %collective-permute-start.1 = (bf16[256,1280]{1,0:T(8,128)(2,1)}, bf16[256,1280]{1,0:T(8,128)(2,1)}, u32[]{:S(2)}, u32[]{:S(2)}) collective-permute-start(bf16[256,1280]{1,0:T(8,128)(2,1)} %fusion.118), channel_id=1, source_target_pairs={{0,2},{1,3},{2,0},{3,1},{4,6},{5,7},{6,4},{7,5},{8,10},{9,11},{10,... | collective-permute-start | bytes 1966088 | tf_op jit(solution)/shard_map/ppermute | solution.py:33
  18.0 1.1 collective-permute-start.2
  19.1 1.4 fusion.178
  20.4 4.0 %fusion.138 = (s32[]{:T(128)}, s32[]{:T(128)}, s32[]{:T(128)}, s32[]{:T(128)}) fusion(s32[1,1024]{1,0:T(1,128)} %param.19, s32[]{:T(128)} %bitcast.17, s32[]{:T(128)} %bitcast.31, s32[]{:T(128)} %bitcast.16, s32[]{:T(128)} %bitcast.32), kind=kLoop, calls=%fused_computation.191 | loop fusion | flops 12284 | bytes 4128 | tf_op jit(solution)/shard_map/reduce_sum | solution.py:71
  31.7 1.4 fusion.194
  33.1 15.6 %collective-permute-done.1 = bf16[256,1280]{1,0:T(8,128)(2,1)} collective-permute-done((bf16[256,1280]{1,0:T(8,128)(2,1)}, bf16[256,1280]{1,0:T(8,128)(2,1)}, u32[]{:S(2)}, u32[]{:S(2)}) %collective-permute-start.1) | collective-permute-done | bytes 655392 | tf_op jit(solution)/shard_map/ppermute | solution.py:33
  48.7 1.6 pad_maximum_fusion
  50.5 2.7 %fusion.106 = bf16[1024,960]{0,1:T(8,128)(2,1)S(1)} fusion(bf16[1280,960]{0,1:T(8,128)(2,1)S(1)} %bitcast.201, bf16[256,1280]{1,0:T(8,128)(2,1)S(1)} %get-tuple-element.327, bf16[256,1280]{1,0:T(8,128)(2,1)S(1)} %get-tuple-element.328, bf16[256,1280]{1,0:T(8,128)(2,1)S(1)} %get-tuple-element.329, bf16[256,1280]{1,0:T(8,128)(2,1)S(1)} %get-tuple-element.326), kind=kOutput, calls=%fused_computation.139 | convolution fusion | flops 2528051200 | bytes 7045120 | tf_op jit(solution)/shard_map/dot_general | solution.py:118
  53.5 1.0 copy-done.4
  54.6 0.7 copy.13
  55.5 0.9 copy.12
  56.4 1.1 fusion.176
  57.5 1.1 copy.14
  58.6 3.1 %while.44 = (s32[]{:T(128)}, f32[4,512]{1,0:T(4,128)S(1)}, f32[4,512]{1,0:T(4,128)S(1)}, s32[]{:T(128)}, s32[512]{0:T(512)S(1)}, /*index=5*/s32[8,128]{1,0:T(8,1...) while((s32[]{:T(128)}, f32[4,512]{1,0:T(4,128)S(1)}, ...), condition=%wide.region_7.8_spmd, body=%wide.region_4.7_spmd.sunk | while | flops 43323396 | bytes 2748055 | solution.py:96
  61.7 9.3 %while.45 = (s32[]{:T(128)}, f32[512,4,80]{0,2,1:T(8,128)S(1)}, s32[]{:T(128)}, bf16[8,128,4,80]{1,3,2,0:T(8,128)(2,1)}, s32[512]{0:T(512)S(1)}, /*index=5*/s32[...) while((s32[]{:T(128)}, f32[512,4,80]{0,2,1:T(8,128)S(1)}, ...), condition=%wide.region_9.10_spmd, body=%wide.region_8.9_spmd.sunk | while | flops 85426176 | bytes 2313899 | solution.py:105
  62.0 2.0 fusion.215
  64.3 2.1 fusion.215
  66.6 2.0 fusion.215
  68.9 2.1 fusion.215
  71.4 3.1 %while.46 = (s32[]{:T(128)}, f32[4,512]{1,0:T(4,128)S(1)}, f32[4,512]{1,0:T(4,128)S(1)}, s32[]{:T(128)}, s32[512]{0:T(512)S(1)}, /*index=5*/s32[8,128]{1,0:T(8,1...) while((s32[]{:T(128)}, f32[4,512]{1,0:T(4,128)S(1)}, ...), condition=%wide.region_15.16_spmd, body=%wide.region_12.15_spmd.sunk | while | flops 43323396 | bytes 2748055 | solution.py:96
  74.6 8.4 %while.47 = (s32[]{:T(128)}, f32[512,4,80]{0,2,1:T(8,128)S(1)}, s32[]{:T(128)}, bf16[8,128,4,80]{1,3,2,0:T(8,128)(2,1)}, s32[512]{0:T(512)S(1)}, /*index=5*/s32[...) while((s32[]{:T(128)}, f32[512,4,80]{0,2,1:T(8,128)S(1)}, ...), condition=%wide.region_17.18_spmd, body=%wide.region_16.17_spmd.sunk | while | flops 85426176 | bytes 2117291 | solution.py:105
  74.8 1.8 fusion.222
  76.9 1.8 fusion.222
  79.0 1.8 fusion.222
  81.1 1.9 fusion.222
  83.1 2.8 %convolution_convert_fusion = bf16[1024,1280]{1,0:T(8,128)(2,1)S(1)} fusion(bf16[320,1280]{1,0:T(8,128)(2,1)} %param.22, bf16[512,320]{0,1:T(8,128)(2,1)S(1)} %bitcast.216, bf16[512,320]{0,1:T(8,128)(2,1)S(1)} %bitcast.215), kind=kOutput, calls=%fused_computation.93 | convolution fusion | flops 841482240 | bytes 4096000 | tf_op jit(solution)/shard_map/dot_general | solution.py:154
  85.9 1.5 copy-done.3
  87.3 1.3 dynamic-slice_bitcast_fusion.6
  88.6 1.1 collective-permute-start.3
  89.7 2.8 %collective-permute-start.4 = (bf16[256,1280]{1,0:T(8,128)(2,1)}, bf16[256,1280]{1,0:T(8,128)(2,1)S(1)}, u32[]{:S(2)}, u32[]{:S(2)}) collective-permute-start(bf16[256,1280]{1,0:T(8,128)(2,1)} %get-tuple-element.325), channel_id=1, source_target_pairs={{0,2},{1,3},{2,0},{3,1},{4,6},{5,7},{6,4},{7,5},{8,10},{9,11},{10,... | collective-permute-start | bytes 1966088 | tf_op jit(solution)/shard_map/ppermute | solution.py:51
  92.9 27.6 %collective-permute-done.3 = bf16[256,1280]{1,0:T(8,128)(2,1)S(1)} collective-permute-done((bf16[256,1280]{1,0:T(8,128)(2,1)}, bf16[256,1280]{1,0:T(8,128)(2,1)S(1)}, u32[]{:S(2)}, u32[]{:S(2)}) %collective-permute-start.3) | collective-permute-done | bytes 655392 | tf_op jit(solution)/shard_map/ppermute | solution.py:51
  120.5 26.8 %collective-permute-done.4 = bf16[256,1280]{1,0:T(8,128)(2,1)S(1)} collective-permute-done((bf16[256,1280]{1,0:T(8,128)(2,1)}, bf16[256,1280]{1,0:T(8,128)(2,1)S(1)}, u32[]{:S(2)}, u32[]{:S(2)}) %collective-permute-start.4) | collective-permute-done | bytes 655392 | tf_op jit(solution)/shard_map/ppermute | solution.py:51
  147.3 1.8 convert_reduce_fusion
  149.5 21.7 %fusion.179 = (f32[256]{0:T(256)S(1)}, f32[256,1280]{1,0:T(8,128)S(1)}) fusion(bf16[2,1280,5120]{1,2,0:T(8,128)(2,1)} %all-gather.2.cloned.1.call-done, bf16[256,1280]{1,0:T(8,128)(2,1)S(1)} %get-tuple-element.318, f32[1280]{0:T(1024)S(1)} %copy-done.7, f32[256]{0:T(256)S(1)} %add_rsqrt_fusion.1, f32[256]{0:T(256)S(1)} %broadcast_multiply_fusion.1), kind=kOutput, calls=%fused_computation.237 | convolution fusion | flops 6798704640 | bytes 28847104 | tf_op jit(solution)/shard_map/dot_general | solution.py:24
  172.3 0.8 collective-permute-start.7
  173.1 1.9 collective-permute-start.8
  175.0 6.1 %fusion.122 = bf16[1,64,1024]{2,1,0:T(8,128)(2,1)S(1)} fusion(bf16[64,5120]{1,0:T(8,128)(2,1)S(1)} %reshape.214, bf16[5120,1024]{1,0:T(8,128)(2,1)} %param.27), kind=kOutput, calls=%fused_computation.160 | convolution fusion | flops 671154176 | bytes 11272192 | tf_op jit(solution)/shard_map/dot_general | solution.py:166
  181.1 22.1 %collective-permute-done.6 = bf16[64,5120]{1,0:T(8,128)(2,1)S(1)} collective-permute-done((bf16[64,5120]{1,0:T(8,128)(2,1)S(1)}, bf16[64,5120]{1,0:T(8,128)(2,1)S(1)}, u32[]{:S(2)}, u32[]{:S(2)}) %collective-permute-start.6) | collective-permute-done | bytes 655392 | tf_op jit(solution)/shard_map/ppermute | solution.py:33
  203.2 5.9 %fusion.123 = bf16[1,64,1024]{2,1,0:T(8,128)(2,1)S(1)} fusion(bf16[64,5120]{1,0:T(8,128)(2,1)S(1)} %collective-permute-done.6, bf16[5120,1024]{1,0:T(8,128)(2,1)} %param.27), kind=kOutput, calls=%fused_computation.161 | convolution fusion | flops 671154176 | bytes 11272192 | tf_op jit(solution)/shard_map/dot_general | solution.py:166
  209.1 2.0 fusion.124
  211.1 1.9 fusion.125
  213.3 19.8 %all_to_all.12 = bf16[32,8,1024]{2,1,0:T(8,128)(2,1)S(1)} all-to-all(bf16[32,8,1024]{2,1,0:T(8,128)(2,1)S(1)} %maximum_bitcast_fusion), channel_id=1, replica_groups=mesh['zx'=16,'core'=2,'tok'=4] {'zx','core'}, dimensions={0} | all-to-all | bytes 1048576 | tf_op jit(solution)/shard_map/all_to_all | solution.py:168
  233.1 0.8 copy.76
  (139 shorter events, 11.0 us)
Async XLA Ops:
  6.5 43.9 %copy-start = (bf16[1280,3,320]{0,2,1:T(8,128)(2,1)S(1)}, bf16[1280,3,320]{0,2,1:T(8,128)(2,1)}, u32[]{:S(2)}) copy-start(bf16[1280,3,320]{0,2,1:T(8,128)(2,1)} %param.21) | copy-start | bytes 7372804
  6.5 143.0 %all-gather.2.cloned.1.call-start = ((), (), s32[]{:S(2)}) async-start(), calls=%async_computation.1 | async-start | bytes 26419200 | tf_op jit(solution)/shard_map/all_gather | solution.py:112
  13.3 19.8 %collective-permute-start = (bf16[256,1280]{1,0:T(8,128)(2,1)}, bf16[256,1280]{1,0:T(8,128)(2,1)S(1)}, u32[]{:S(2)}, u32[]{:S(2)}) collective-permute-start(bf16[256,1280]{1,0:T(8,128)(2,1)} %fusion.118), channel_id=1, source_target_pairs={{0,1},{1,2},{2,3},{3,0},{4,5},{5,6},{6,7},{7,4},{8,9},{9,10},{10,1... | collective-permute-start | bytes 1966088 | tf_op jit(solution)/shard_map/ppermute | solution.py:33
  15.4 33.3 %collective-permute-start.1 = (bf16[256,1280]{1,0:T(8,128)(2,1)}, bf16[256,1280]{1,0:T(8,128)(2,1)}, u32[]{:S(2)}, u32[]{:S(2)}) collective-permute-start(bf16[256,1280]{1,0:T(8,128)(2,1)} %fusion.118), channel_id=1, source_target_pairs={{0,2},{1,3},{2,0},{3,1},{4,6},{5,7},{6,4},{7,5},{8,10},{9,11},{10,... | collective-permute-start | bytes 1966088 | tf_op jit(solution)/shard_map/ppermute | solution.py:33
  18.0 30.7 %collective-permute-start.2 = (bf16[256,1280]{1,0:T(8,128)(2,1)}, bf16[256,1280]{1,0:T(8,128)(2,1)}, u32[]{:S(2)}, u32[]{:S(2)}) collective-permute-start(bf16[256,1280]{1,0:T(8,128)(2,1)} %fusion.118), channel_id=1, source_target_pairs={{0,3},{1,0},{2,1},{3,2},{4,7},{5,4},{6,5},{7,6},{8,11},{9,8},{10,9... | collective-permute-start | bytes 1966088 | tf_op jit(solution)/shard_map/ppermute | solution.py:33
  53.2 1.3 copy-start.4
  53.2 5.3 %copy-start.5 = (s32[1,1024]{1,0:T(1,128)S(1)}, s32[1,1024]{1,0:T(1,128)}, u32[]{:S(2)}) copy-start(s32[1,1024]{1,0:T(1,128)} %param.19) | copy-start | bytes 12292
  83.1 64.3 %copy-start.2 = (bf16[256,1280]{1,0:T(8,128)(2,1)S(1)}, bf16[256,1280]{1,0:T(8,128)(2,1)}, u32[]{:S(2)}) copy-start(bf16[256,1280]{1,0:T(8,128)(2,1)} %param.18) | copy-start | bytes 1966084
  85.8 1.5 copy-start.3
  85.8 63.7 %copy-start.7 = (f32[1280]{0:T(1024)S(1)}, f32[1280]{0:T(1024)}, u32[]{:S(2)}) copy-start(f32[1280]{0:T(1024)} %param.23) | copy-start | bytes 15364
  88.6 31.9 %collective-permute-start.3 = (bf16[256,1280]{1,0:T(8,128)(2,1)}, bf16[256,1280]{1,0:T(8,128)(2,1)S(1)}, u32[]{:S(2)}, u32[]{:S(2)}) collective-permute-start(bf16[256,1280]{1,0:T(8,128)(2,1)} %get-tuple-element.323), channel_id=1, source_target_pairs={{0,1},{1,2},{2,3},{3,0},{4,5},{5,6},{6,7},{7,4},{8,9},{9,10},{10,1... | collective-permute-start | bytes 1966088 | tf_op jit(solution)/shard_map/ppermute | solution.py:51
  89.7 57.6 %collective-permute-start.4 = (bf16[256,1280]{1,0:T(8,128)(2,1)}, bf16[256,1280]{1,0:T(8,128)(2,1)S(1)}, u32[]{:S(2)}, u32[]{:S(2)}) collective-permute-start(bf16[256,1280]{1,0:T(8,128)(2,1)} %get-tuple-element.325), channel_id=1, source_target_pairs={{0,2},{1,3},{2,0},{3,1},{4,6},{5,7},{6,4},{7,5},{8,10},{9,11},{10,... | collective-permute-start | bytes 1966088 | tf_op jit(solution)/shard_map/ppermute | solution.py:51
  92.5 54.8 %collective-permute-start.5 = (bf16[256,1280]{1,0:T(8,128)(2,1)S(1)}, bf16[256,1280]{1,0:T(8,128)(2,1)}, u32[]{:S(2)}, u32[]{:S(2)}) collective-permute-start(bf16[256,1280]{1,0:T(8,128)(2,1)S(1)} %get-tuple-element.324), channel_id=1, source_target_pairs={{0,3},{1,0},{2,1},{3,2},{4,7},{5,4},{6,5},{7,6},{8,11},{9,8},{10,9... | collective-permute-start | bytes 1966088 | tf_op jit(solution)/shard_map/ppermute | solution.py:51
  149.5 22.1 %copy-start.6 = (f32[1280]{0:T(1024)S(1)}, f32[1280]{0:T(1024)}, u32[]{:S(2)}) copy-start(f32[1280]{0:T(1024)} %param.26) | copy-start | bytes 15364
  172.2 30.9 %collective-permute-start.6 = (bf16[64,5120]{1,0:T(8,128)(2,1)S(1)}, bf16[64,5120]{1,0:T(8,128)(2,1)S(1)}, u32[]{:S(2)}, u32[]{:S(2)}) collective-permute-start(bf16[64,5120]{1,0:T(8,128)(2,1)S(1)} %reshape.214), channel_id=1, source_target_pairs={{0,1},{1,2},{2,3},{3,0},{4,5},{5,6},{6,7},{7,4},{8,9},{9,10},{10,1... | collective-permute-start | bytes 1966088 | tf_op jit(solution)/shard_map/ppermute | solution.py:33
  172.3 36.8 %collective-permute-start.7 = (bf16[64,5120]{1,0:T(8,128)(2,1)S(1)}, bf16[64,5120]{1,0:T(8,128)(2,1)S(1)}, u32[]{:S(2)}, u32[]{:S(2)}) collective-permute-start(bf16[64,5120]{1,0:T(8,128)(2,1)S(1)} %reshape.214), channel_id=1, source_target_pairs={{0,2},{1,3},{2,0},{3,1},{4,6},{5,7},{6,4},{7,5},{8,10},{9,11},{10,... | collective-permute-start | bytes 1966088 | tf_op jit(solution)/shard_map/ppermute | solution.py:33
  173.1 38.0 %collective-permute-start.8 = (bf16[64,5120]{1,0:T(8,128)(2,1)S(1)}, bf16[64,5120]{1,0:T(8,128)(2,1)S(1)}, u32[]{:S(2)}, u32[]{:S(2)}) collective-permute-start(bf16[64,5120]{1,0:T(8,128)(2,1)S(1)} %reshape.214), channel_id=1, source_target_pairs={{0,3},{1,0},{2,1},{3,2},{4,7},{5,4},{6,5},{7,6},{8,11},{9,8},{10,9... | collective-permute-start | bytes 1966088 | tf_op jit(solution)/shard_map/ppermute | solution.py:33
  175.0 34.1 %slice-start = ((s8[10485760]{0:T(1024)(128)(4,1)}), s8[4194304]{0:T(1024)(128)(4,1)S(1)}, s32[]{:S(2)}) async-start(s8[10485760]{0:T(1024)(128)(4,1)} %bitcast.202), calls=%async_computation.2 | async-start | bytes 8388608
  175.0 34.1 %slice-start.1 = ((s8[10485760]{0:T(1024)(128)(4,1)}), s8[4194304]{0:T(1024)(128)(4,1)S(1)}, s32[]{:S(2)}) async-start(s8[10485760]{0:T(1024)(128)(4,1)} %bitcast.202), calls=%async_computation.3 | async-start | bytes 8388608
  181.0 28.1 %slice-start.2 = ((s8[10485760]{0:T(1024)(128)(4,1)}), s8[2097152]{0:T(1024)(128)(4,1)S(1)}, s32[]{:S(2)}) async-start(s8[10485760]{0:T(1024)(128)(4,1)} %bitcast.202), calls=%async_computation.4 | async-start | bytes 4194304
  211.1 22.7 %copy-start.1 = (bf16[1280,3,320]{0,2,1:T(8,128)(2,1)S(1)}, bf16[1280,3,320]{0,2,1:T(8,128)(2,1)}, u32[]{:S(2)}) copy-start(bf16[1280,3,320]{0,2,1:T(8,128)(2,1)} %param.21) | copy-start | bytes 7372804
Sparse Core Ops, SparseCore 0:
  10.3 135.7 all-gather.1

commit v4 on v1

--- a/solution.py
+++ b/solution.py
@@ -26,13 +26,23 @@
     )
 
 
+def shift(rows, axis, count, s):
+    return lax.ppermute(rows, axis, [(i, (i + s) % count) for i in range(count)])
+
+
+def shift_rows(rows, axis, count, s):
+    if count != 4 or s != 2:
+        return shift(rows, axis, count, s)
+    half = rows.shape[0] // 2
+    ahead = shift(rows[:half], axis, count, 2)
+    behind = shift(shift(rows[half:], axis, count, -1), axis, count, -1)
+    return jnp.concatenate([ahead, behind], axis=0)
+
+
 def permute_gather(rows, axis):
     count = lax.axis_size(axis)
     here = lax.axis_index(axis)
-    shifted = [rows] + [
-        lax.ppermute(rows, axis, [(i, (i + s) % count) for i in range(count)])
-        for s in range(1, count)
-    ]
+    shifted = [rows] + [shift_rows(rows, axis, count, s) for s in range(1, count)]
     stacked = jnp.stack(shifted)
     blocks = [
         lax.dynamic_index_in_dim(stacked, (here - source) % count, axis=0, keepdims=False)
@@ -48,7 +58,7 @@
     total = lax.dynamic_index_in_dim(blocks, here, axis=0, keepdims=False).astype(jnp.float32)
     for s in range(1, count):
         outgoing = lax.dynamic_index_in_dim(blocks, (here + s) % count, axis=0, keepdims=False)
-        incoming = lax.ppermute(outgoing, axis, [(i, (i + s) % count) for i in range(count)])
+        incoming = shift_rows(outgoing, axis, count, s)
         total = total + incoming.astype(jnp.float32)
     return total
 

time: 248 us -> 259 us (1.044)
  starting transfers between devices: 12.5 us -> 24.6 us
  waiting for transfers between devices: 83.7 us -> 77 us
  blocking collectives: 20 us -> 23.4 us
    ppermute x9 -> x15, starting transfers between devices: 12.5 us -> 24.6 us  [shift(): lax.ppermute(rows, axis, [(i, (i + s) % count) for i in range(count)])]
    ppermute x9 -> x15, waiting for transfers between devices: 83.7 us -> 76.9 us  [shift(): lax.ppermute(rows, axis, [(i, (i + s) % count) for i in range(count)])]
    slice x0 -> x5, local copies, waits for them, and re-layouts: none -> 3.79 us  [the longest x4 3.58 us: shift_rows(): ahead = shift(rows[:half], axis, count, 2)]
    all_to_all x1, blocking collectives: 20 us -> 23.4 us  [layer(): lax.all_to_all(projected, ('zx', 'core'), split_axis=0, concat_axis=0, ti...]
    another operation x3 -> x5, other arithmetic: 3.3 us -> 5.56 us  [permute_gather(): stacked = jnp.stack(shifted)]
  transfers between devices with their start and end apart: 10 -> 16, of which waited for: 5 -> 8; matrix products, arithmetic and copies ran while one was open for 28% -> 29% of each run, Pallas kernels for 0% -> 0%
where the time goes in v4:
time: 259 us; the launch traced here: 257 us
  waiting for transfers between devices  77 us (30%)
  matrix products  56.5 us (22%)
  other arithmetic  29.8 us (12%)
  local copies, waits for them, and re-layouts  24.8 us (10%)
  starting transfers between devices  24.6 us (9%)
  blocking collectives  23.4 us (9%)
  between operations  20.1 us (8%)
    ppermute x15, waiting for transfers between devices, shift(): lax.ppermute(rows, axis, [(i, (i + s) % count) for i in range(count)])  76.9 us
    dot_general x1, matrix products, hidden_fold(): lax.dot_general(hidden, down_piece, (((1,), (1,)), ((), ())), preferred_e...  25.7 us
    ppermute x15, starting transfers between devices, shift(): lax.ppermute(rows, axis, [(i, (i + s) % count) for i in range(count)])  24.6 us
    all_to_all x1, blocking collectives, layer(): lax.all_to_all(projected, ('zx', 'core'), split_axis=0, concat_axis=0, ti...  23.4 us
    dot_general x8, matrix products, add_values(): jnp.einsum('hqk,khd->qhd', weights, values_blocked[kblock], preferred_ele...  14.9 us
    dynamic_slice x16, local copies, waits for them, and re-layouts, block_scores(): same = query_images[:, None] == images_blocked[kblock][None, :]  11.2 us
    eq x16, other arithmetic, block_scores(): same = query_images[:, None] == images_blocked[kblock][None, :]  7.38 us
    dot_general x1, matrix products, layer(): jnp.dot(permute_gather(merged, 'tok'), w_proj, preferred_element_type=jnp...  7.06 us
  transfers between devices with their start and end apart: 16, of which 8 were waited for; matrix products, arithmetic and copies ran while one was open for 29% of the time, Pallas kernels for 0%

profile of v4, /device:TPU:1, one launch (start us, length us, event | category | flops | bytes accessed | tf_op | source)
XLA Modules:
  0.0 257.1 jit_solution(7404322970105352202)
XLA Ops:
  6.5 1.8 pad_maximum_fusion.2
  8.4 1.3 convert_reduce_fusion.1
  9.6 1.4 fusion.124
  11.1 2.2 fusion.126
  13.3 2.1 collective-permute-start
  15.4 1.4 collective-permute-start.4
  16.8 1.8 fusion.189
  18.7 1.5 collective-permute-start.2
  20.5 1.4 fusion.200
  22.5 17.7 %collective-permute-done.2 = bf16[128,1280]{1,0:T(8,128)(2,1)} collective-permute-done((bf16[128,1280]{1,0:T(8,128)(2,1)}, bf16[128,1280]{1,0:T(8,128)(2,1)}, u32[]{:S(2)}, u32[]{:S(2)}) %collective-permute-start.2) | collective-permute-done | bytes 327712 | tf_op jit(solution)/shard_map/ppermute | solution.py:30
  40.2 3.2 %collective-permute-start.3 = (bf16[128,1280]{1,0:T(8,128)(2,1)}, bf16[128,1280]{1,0:T(8,128)(2,1)}, u32[]{:S(2)}, u32[]{:S(2)}) collective-permute-start(bf16[128,1280]{1,0:T(8,128)(2,1)} %collective-permute-done.2), channel_id=1, source_target_pairs={{0,3},{1,0},{2,1},{3,2},{4,7},{5,4},{6,5},{7,6},{8,11},{9,8},{10,9... | collective-permute-start | bytes 983048 | tf_op jit(solution)/shard_map/ppermute | solution.py:30
  43.5 3.1 %fusion.148 = (s32[]{:T(128)}, s32[]{:T(128)}, s32[]{:T(128)}, s32[]{:T(128)}) fusion(s32[1,1024]{1,0:T(1,128)S(1)} %copy-done.5, s32[]{:T(128)} %bitcast.17, s32[]{:T(128)} %bitcast.31, s32[]{:T(128)} %bitcast.16, s32[]{:T(128)} %bitcast.32), kind=kLoop, calls=%fused_computation.195 | loop fusion | flops 12284 | bytes 4128 | tf_op jit(solution)/shard_map/reduce_sum | solution.py:81
  53.4 4.2 %collective-permute-done.3 = bf16[128,1280]{1,0:T(8,128)(2,1)} collective-permute-done((bf16[128,1280]{1,0:T(8,128)(2,1)}, bf16[128,1280]{1,0:T(8,128)(2,1)}, u32[]{:S(2)}, u32[]{:S(2)}) %collective-permute-start.3) | collective-permute-done | bytes 327712 | tf_op jit(solution)/shard_map/ppermute | solution.py:30
  57.6 1.1 maximum_bitcast_fusion
  58.7 1.6 pad_maximum_fusion
  60.6 2.7 %fusion.114 = bf16[1024,960]{0,1:T(8,128)(2,1)S(1)} fusion(bf16[1280,960]{0,1:T(8,128)(2,1)S(1)} %bitcast.193, bf16[256,1280]{1,0:T(8,128)(2,1)S(1)} %get-tuple-element.332, bf16[256,1280]{1,0:T(8,128)(2,1)S(1)} %get-tuple-element.333, bf16[256,1280]{1,0:T(8,128)(2,1)S(1)} %get-tuple-element.334, bf16[256,1280]{1,0:T(8,128)(2,1)S(1)} %get-tuple-element.331), kind=kOutput, calls=%fused_computation.148 | convolution fusion | flops 2528051200 | bytes 7045120 | tf_op jit(solution)/shard_map/dot_general | solution.py:128
  66.5 1.1 fusion.187
  67.9 8.5 %while.44 = (s32[]{:T(128)}, f32[4,512]{1,0:T(4,128)S(1)}, f32[4,512]{1,0:T(4,128)S(1)}, s32[]{:T(128)}, s32[512]{0:T(512)}, /*index=5*/s32[8,128]{1,0:T(8,128)}...) while((s32[]{:T(128)}, f32[4,512]{1,0:T(4,128)S(1)}, ...), condition=%wide.region_7.8_spmd, body=%wide.region_4.7_spmd.sunk | while | flops 43323396 | bytes 2748055 | solution.py:106
  76.6 14.0 %while.45 = (s32[]{:T(128)}, f32[512,4,80]{0,2,1:T(8,128)S(1)}, s32[]{:T(128)}, bf16[8,128,4,80]{1,3,2,0:T(8,128)(2,1)}, s32[512]{0:T(512)}, /*index=5*/s32[8,12...) while((s32[]{:T(128)}, f32[512,4,80]{0,2,1:T(8,128)S(1)}, ...), condition=%wide.region_9.10_spmd, body=%wide.region_8.9_spmd.sunk | while | flops 85426176 | bytes 2117291 | solution.py:115
  78.2 1.9 fusion.221
  81.7 1.9 fusion.221
  85.1 1.9 fusion.221
  88.6 1.9 fusion.221
  91.6 5.8 %while.46 = (s32[]{:T(128)}, f32[4,512]{1,0:T(4,128)S(1)}, f32[4,512]{1,0:T(4,128)S(1)}, s32[]{:T(128)}, s32[512]{0:T(512)S(1)}, /*index=5*/s32[8,128]{1,0:T(8,1...) while((s32[]{:T(128)}, f32[4,512]{1,0:T(4,128)S(1)}, ...), condition=%wide.region_15.16_spmd, body=%wide.region_12.15_spmd.sunk | while | flops 43323396 | bytes 2748055 | solution.py:106
  97.5 11.3 %while.47 = (s32[]{:T(128)}, f32[512,4,80]{0,2,1:T(8,128)S(1)}, s32[]{:T(128)}, bf16[8,128,4,80]{1,3,2,0:T(8,128)(2,1)}, s32[512]{0:T(512)S(1)}, /*index=5*/s32[...) while((s32[]{:T(128)}, f32[512,4,80]{0,2,1:T(8,128)S(1)}, ...), condition=%wide.region_17.18_spmd, body=%wide.region_16.17_spmd.sunk | while | flops 85426176 | bytes 2117291 | solution.py:115
  98.5 1.8 fusion.228
  101.2 1.8 fusion.228
  104.0 1.8 fusion.228
  106.8 1.8 fusion.228
  108.9 2.9 %convolution_convert_fusion = bf16[1024,1280]{1,0:T(8,128)(2,1)S(1)} fusion(bf16[320,1280]{1,0:T(8,128)(2,1)} %param.22, bf16[512,320]{0,1:T(8,128)(2,1)S(1)} %bitcast.208, bf16[512,320]{0,1:T(8,128)(2,1)} %bitcast.207), kind=kOutput, calls=%fused_computation.93 | convolution fusion | flops 841482240 | bytes 4096000 | tf_op jit(solution)/shard_map/dot_general | solution.py:164
  111.9 1.1 dynamic-slice_bitcast_fusion.9
  113.0 4.2 %collective-permute-start.5 = (bf16[256,1280]{1,0:T(8,128)(2,1)}, bf16[256,1280]{1,0:T(8,128)(2,1)}, u32[]{:S(2)}, u32[]{:S(2)}) collective-permute-start(bf16[256,1280]{1,0:T(8,128)(2,1)} %get-tuple-element.327), channel_id=1, source_target_pairs={{0,1},{1,2},{2,3},{3,0},{4,5},{5,6},{6,7},{7,4},{8,9},{9,10},{10,1... | collective-permute-start | bytes 1966088 | tf_op jit(solution)/shard_map/ppermute | solution.py:30
  118.3 2.9 %collective-permute-start.6 = (bf16[128,1280]{1,0:T(8,128)(2,1)}, bf16[128,1280]{1,0:T(8,128)(2,1)}, u32[]{:S(2)}, u32[]{:S(2)}) collective-permute-start(bf16[128,1280]{1,0:T(8,128)(2,1)} %get-tuple-element.329), channel_id=1, source_target_pairs={{0,2},{1,3},{2,0},{3,1},{4,6},{5,7},{6,4},{7,5},{8,10},{9,11},{10,... | collective-permute-start | bytes 983048 | tf_op jit(solution)/shard_map/ppermute | solution.py:30
  121.2 17.3 %collective-permute-done.7 = bf16[128,1280]{1,0:T(8,128)(2,1)} collective-permute-done((bf16[128,1280]{1,0:T(8,128)(2,1)S(1)}, bf16[128,1280]{1,0:T(8,128)(2,1)}, u32[]{:S(2)}, u32[]{:S(2)}) %collective-permute-start.7) | collective-permute-done | bytes 327712 | tf_op jit(solution)/shard_map/ppermute | solution.py:30
  138.6 13.0 %collective-permute-done.8 = bf16[128,1280]{1,0:T(8,128)(2,1)} collective-permute-done((bf16[128,1280]{1,0:T(8,128)(2,1)}, bf16[128,1280]{1,0:T(8,128)(2,1)}, u32[]{:S(2)}, u32[]{:S(2)}) %collective-permute-start.8) | collective-permute-done | bytes 327712 | tf_op jit(solution)/shard_map/ppermute | solution.py:30
  151.6 2.8 %convert_reduce_fusion = (f32[256]{0:T(256)S(1)}, bf16[256,1280]{1,0:T(8,128)(2,1)}) fusion(bf16[256,1280]{1,0:T(8,128)(2,1)} %collective-permute-done.9, bf16[128,1280]{1,0:T(8,128)(2,1)} %collective-permute-done.8, bf16[128,1280]{1,0:T(8,128)(2,1)} %collective-permute-done.6, bf16[256,1280]{1,0:T(8,128)(2,1)} %collective-permute-done.5, ...), kind=kLoop, calls=%fused_computation.144 | loop fusion | flops 4914944 | bytes 3933188 | tf_op jit(solution)/shard_map/reduce_sum | solution.py:13
  154.4 1.4 fusion.121
  155.9 25.7 %fusion.192 = (f32[256]{0:T(256)S(1)}, f32[256,1280]{1,0:T(8,128)S(1)}) fusion(bf16[2,1280,5120]{1,2,0:T(8,128)(2,1)} %all-gather.2.cloned.1.call-done, bf16[256,1280]{1,0:T(8,128)(2,1)} %get-tuple-element.318, f32[1280]{0:T(1024)S(1)} %copy-done.7, f32[256]{0:T(256)S(1)} %add_rsqrt_fusion.1, f32[256]{0:T(256)S(1)} %broadcast_multiply_fusion.1), kind=kOutput, calls=%fused_computation.244 | convolution fusion | flops 6798704640 | bytes 28844032 | tf_op jit(solution)/shard_map/dot_general | solution.py:24
  182.4 2.1 collective-permute-start.12
  185.5 7.2 %collective-permute-done.12 = bf16[32,5120]{1,0:T(8,128)(2,1)} collective-permute-done((bf16[32,5120]{1,0:T(8,128)(2,1)S(1)}, bf16[32,5120]{1,0:T(8,128)(2,1)}, u32[]{:S(2)}, u32[]{:S(2)}) %collective-permute-start.12) | collective-permute-done | bytes 327712 | tf_op jit(solution)/shard_map/ppermute | solution.py:30
  192.7 3.7 %collective-permute-start.13 = (bf16[32,5120]{1,0:T(8,128)(2,1)}, bf16[32,5120]{1,0:T(8,128)(2,1)}, u32[]{:S(2)}, u32[]{:S(2)}) collective-permute-start(bf16[32,5120]{1,0:T(8,128)(2,1)} %collective-permute-done.12), channel_id=1, source_target_pairs={{0,3},{1,0},{2,1},{3,2},{4,7},{5,4},{6,5},{7,6},{8,11},{9,8},{10,9... | collective-permute-start | bytes 983048 | tf_op jit(solution)/shard_map/ppermute | solution.py:30
  196.8 2.7 %collective-permute-start.14 = (bf16[64,5120]{1,0:T(8,128)(2,1)S(1)}, bf16[64,5120]{1,0:T(8,128)(2,1)S(1)}, u32[]{:S(2)}, u32[]{:S(2)}) collective-permute-start(bf16[64,5120]{1,0:T(8,128)(2,1)S(1)} %reshape.218), channel_id=1, source_target_pairs={{0,3},{1,0},{2,1},{3,2},{4,7},{5,4},{6,5},{7,6},{8,11},{9,8},{10,9... | collective-permute-start | bytes 1966088 | tf_op jit(solution)/shard_map/ppermute | solution.py:30
  199.9 4.6 %collective-permute-done.13 = bf16[32,5120]{1,0:T(8,128)(2,1)} collective-permute-done((bf16[32,5120]{1,0:T(8,128)(2,1)}, bf16[32,5120]{1,0:T(8,128)(2,1)}, u32[]{:S(2)}, u32[]{:S(2)}) %collective-permute-start.13) | collective-permute-done | bytes 327712 | tf_op jit(solution)/shard_map/ppermute | solution.py:30
  204.5 1.1 maximum_bitcast_fusion.1
  205.6 3.0 %collective-permute-done.10 = bf16[64,5120]{1,0:T(8,128)(2,1)S(1)} collective-permute-done((bf16[64,5120]{1,0:T(8,128)(2,1)S(1)}, bf16[64,5120]{1,0:T(8,128)(2,1)S(1)}, u32[]{:S(2)}, u32[]{:S(2)}) %collective-permute-start.10) | collective-permute-done | bytes 655392 | tf_op jit(solution)/shard_map/ppermute | solution.py:30
  208.6 9.8 %collective-permute-done.14 = bf16[64,5120]{1,0:T(8,128)(2,1)S(1)} collective-permute-done((bf16[64,5120]{1,0:T(8,128)(2,1)S(1)}, bf16[64,5120]{1,0:T(8,128)(2,1)S(1)}, u32[]{:S(2)}, u32[]{:S(2)}) %collective-permute-start.14) | collective-permute-done | bytes 655392 | tf_op jit(solution)/shard_map/ppermute | solution.py:30
  219.0 7.1 %fusion.133 = bf16[32,8,1024]{2,1,0:T(8,128)(2,1)S(1)} fusion(bf16[5120,1024]{1,0:T(8,128)(2,1)} %param.27, bf16[64,5120]{1,0:T(8,128)(2,1)S(1)} %get-tuple-element.324, bf16[64,5120]{1,0:T(8,128)(2,1)S(1)} %get-tuple-element.325, bf16[64,5120]{1,0:T(8,128)(2,1)S(1)} %get-tuple-element.326, bf16[64,5120]{1,0:T(8,128)(2,1)S(1)} %get-tuple-element.323), kind=kOutput, calls=%fused_computation.166 | convolution fusion | flops 2695102464 | bytes 13631488 | tf_op jit(solution)/shard_map/dot_general | solution.py:173
  226.0 23.4 %all_to_all.12 = bf16[32,8,1024]{2,1,0:T(8,128)(2,1)S(1)} all-to-all(bf16[32,8,1024]{2,1,0:T(8,128)(2,1)S(1)} %fusion.133), channel_id=1, replica_groups=mesh['zx'=16,'core'=2,'tok'=4] {'zx','core'}, dimensions={0} | all-to-all | bytes 1048576 | tf_op jit(solution)/shard_map/all_to_all | solution.py:178
  (148 shorter events, 35.2 us)
Async XLA Ops:
  6.5 54.0 %copy-start = (bf16[1280,3,320]{0,2,1:T(8,128)(2,1)S(1)}, bf16[1280,3,320]{0,2,1:T(8,128)(2,1)}, u32[]{:S(2)}) copy-start(bf16[1280,3,320]{0,2,1:T(8,128)(2,1)} %param.21) | copy-start | bytes 7372804
  6.5 15.4 %copy-start.5 = (s32[1,1024]{1,0:T(1,128)S(1)}, s32[1,1024]{1,0:T(1,128)}, u32[]{:S(2)}) copy-start(s32[1,1024]{1,0:T(1,128)} %param.19) | copy-start | bytes 12292
  6.5 149.3 %all-gather.2.cloned.1.call-start = ((), (), s32[]{:S(2)}) async-start(), calls=%async_computation.1 | async-start | bytes 26419200 | tf_op jit(solution)/shard_map/all_gather | solution.py:122
  13.3 45.5 %collective-permute-start = (bf16[256,1280]{1,0:T(8,128)(2,1)}, bf16[256,1280]{1,0:T(8,128)(2,1)}, u32[]{:S(2)}, u32[]{:S(2)}) collective-permute-start(bf16[256,1280]{1,0:T(8,128)(2,1)} %fusion.126), channel_id=1, source_target_pairs={{0,1},{1,2},{2,3},{3,0},{4,5},{5,6},{6,7},{7,4},{8,9},{9,10},{10,1... | collective-permute-start | bytes 1966088 | tf_op jit(solution)/shard_map/ppermute | solution.py:30
  15.4 43.3 %collective-permute-start.4 = (bf16[256,1280]{1,0:T(8,128)(2,1)}, bf16[256,1280]{1,0:T(8,128)(2,1)}, u32[]{:S(2)}, u32[]{:S(2)}) collective-permute-start(bf16[256,1280]{1,0:T(8,128)(2,1)} %fusion.126), channel_id=1, source_target_pairs={{0,3},{1,0},{2,1},{3,2},{4,7},{5,4},{6,5},{7,6},{8,11},{9,8},{10,9... | collective-permute-start | bytes 1966088 | tf_op jit(solution)/shard_map/ppermute | solution.py:30
  18.7 21.6 %collective-permute-start.2 = (bf16[128,1280]{1,0:T(8,128)(2,1)}, bf16[128,1280]{1,0:T(8,128)(2,1)}, u32[]{:S(2)}, u32[]{:S(2)}) collective-permute-start(bf16[128,1280]{1,0:T(8,128)(2,1)} %get-tuple-element.342), channel_id=1, source_target_pairs={{0,3},{1,0},{2,1},{3,2},{4,7},{5,4},{6,5},{7,6},{8,11},{9,8},{10,9... | collective-permute-start | bytes 983048 | tf_op jit(solution)/shard_map/ppermute | solution.py:30
  20.1 33.2 %collective-permute-start.1 = (bf16[128,1280]{1,0:T(8,128)(2,1)S(1)}, bf16[128,1280]{1,0:T(8,128)(2,1)}, u32[]{:S(2)}, u32[]{:S(2)}) collective-permute-start(bf16[128,1280]{1,0:T(8,128)(2,1)S(1)} %get-tuple-element.341), channel_id=1, source_target_pairs={{0,2},{1,3},{2,0},{3,1},{4,6},{5,7},{6,4},{7,5},{8,10},{9,11},{10,... | collective-permute-start | bytes 983048 | tf_op jit(solution)/shard_map/ppermute | solution.py:30
  40.2 17.4 %collective-permute-start.3 = (bf16[128,1280]{1,0:T(8,128)(2,1)}, bf16[128,1280]{1,0:T(8,128)(2,1)}, u32[]{:S(2)}, u32[]{:S(2)}) collective-permute-start(bf16[128,1280]{1,0:T(8,128)(2,1)} %collective-permute-done.2), channel_id=1, source_target_pairs={{0,3},{1,0},{2,1},{3,2},{4,7},{5,4},{6,5},{7,6},{8,11},{9,8},{10,9... | collective-permute-start | bytes 983048 | tf_op jit(solution)/shard_map/ppermute | solution.py:30
  63.3 1.3 copy-start.3
  76.5 15.1 %copy-start.4 = (s32[1,512]{1,0:T(1,128)S(1)}, s32[1,512]{1,0:T(1,128)}, u32[]{:S(2)}) copy-start(s32[1,512]{1,0:T(1,128)} %get-tuple-element.344) | copy-start | bytes 6148
  108.9 42.7 %copy-start.2 = (bf16[256,1280]{1,0:T(8,128)(2,1)S(1)}, bf16[256,1280]{1,0:T(8,128)(2,1)}, u32[]{:S(2)}) copy-start(bf16[256,1280]{1,0:T(8,128)(2,1)} %param.18) | copy-start | bytes 1966084
  111.9 44.0 %copy-start.7 = (f32[1280]{0:T(1024)S(1)}, f32[1280]{0:T(1024)}, u32[]{:S(2)}) copy-start(f32[1280]{0:T(1024)} %param.23) | copy-start | bytes 15364
  113.0 25.6 %collective-permute-start.5 = (bf16[256,1280]{1,0:T(8,128)(2,1)}, bf16[256,1280]{1,0:T(8,128)(2,1)}, u32[]{:S(2)}, u32[]{:S(2)}) collective-permute-start(bf16[256,1280]{1,0:T(8,128)(2,1)} %get-tuple-element.327), channel_id=1, source_target_pairs={{0,1},{1,2},{2,3},{3,0},{4,5},{5,6},{6,7},{7,4},{8,9},{9,10},{10,1... | collective-permute-start | bytes 1966088 | tf_op jit(solution)/shard_map/ppermute | solution.py:30
  117.2 21.4 %collective-permute-start.9 = (bf16[256,1280]{1,0:T(8,128)(2,1)}, bf16[256,1280]{1,0:T(8,128)(2,1)}, u32[]{:S(2)}, u32[]{:S(2)}) collective-permute-start(bf16[256,1280]{1,0:T(8,128)(2,1)} %get-tuple-element.328), channel_id=1, source_target_pairs={{0,3},{1,0},{2,1},{3,2},{4,7},{5,4},{6,5},{7,6},{8,11},{9,8},{10,9... | collective-permute-start | bytes 1966088 | tf_op jit(solution)/shard_map/ppermute | solution.py:30
  118.0 20.6 %collective-permute-start.7 = (bf16[128,1280]{1,0:T(8,128)(2,1)S(1)}, bf16[128,1280]{1,0:T(8,128)(2,1)}, u32[]{:S(2)}, u32[]{:S(2)}) collective-permute-start(bf16[128,1280]{1,0:T(8,128)(2,1)S(1)} %get-tuple-element.330), channel_id=1, source_target_pairs={{0,3},{1,0},{2,1},{3,2},{4,7},{5,4},{6,5},{7,6},{8,11},{9,8},{10,9... | collective-permute-start | bytes 983048 | tf_op jit(solution)/shard_map/ppermute | solution.py:30
  118.3 20.3 %collective-permute-start.6 = (bf16[128,1280]{1,0:T(8,128)(2,1)}, bf16[128,1280]{1,0:T(8,128)(2,1)}, u32[]{:S(2)}, u32[]{:S(2)}) collective-permute-start(bf16[128,1280]{1,0:T(8,128)(2,1)} %get-tuple-element.329), channel_id=1, source_target_pairs={{0,2},{1,3},{2,0},{3,1},{4,6},{5,7},{6,4},{7,5},{8,10},{9,11},{10,... | collective-permute-start | bytes 983048 | tf_op jit(solution)/shard_map/ppermute | solution.py:30
  138.6 13.0 %collective-permute-start.8 = (bf16[128,1280]{1,0:T(8,128)(2,1)}, bf16[128,1280]{1,0:T(8,128)(2,1)}, u32[]{:S(2)}, u32[]{:S(2)}) collective-permute-start(bf16[128,1280]{1,0:T(8,128)(2,1)} %collective-permute-done.7), channel_id=1, source_target_pairs={{0,3},{1,0},{2,1},{3,2},{4,7},{5,4},{6,5},{7,6},{8,11},{9,8},{10,9... | collective-permute-start | bytes 983048 | tf_op jit(solution)/shard_map/ppermute | solution.py:30
  155.8 26.1 %copy-start.6 = (f32[1280]{0:T(1024)S(1)}, f32[1280]{0:T(1024)}, u32[]{:S(2)}) copy-start(f32[1280]{0:T(1024)} %param.26) | copy-start | bytes 15364
  182.4 10.3 %collective-permute-start.12 = (bf16[32,5120]{1,0:T(8,128)(2,1)S(1)}, bf16[32,5120]{1,0:T(8,128)(2,1)}, u32[]{:S(2)}, u32[]{:S(2)}) collective-permute-start(bf16[32,5120]{1,0:T(8,128)(2,1)S(1)} %slice.102), channel_id=1, source_target_pairs={{0,3},{1,0},{2,1},{3,2},{4,7},{5,4},{6,5},{7,6},{8,11},{9,8},{10,9... | collective-permute-start | bytes 983048 | tf_op jit(solution)/shard_map/ppermute | solution.py:30
  185.5 14.4 %collective-permute-start.11 = (bf16[32,5120]{1,0:T(8,128)(2,1)}, bf16[32,5120]{1,0:T(8,128)(2,1)}, u32[]{:S(2)}, u32[]{:S(2)}) collective-permute-start(bf16[32,5120]{1,0:T(8,128)(2,1)} %slice.100), channel_id=1, source_target_pairs={{0,2},{1,3},{2,0},{3,1},{4,6},{5,7},{6,4},{7,5},{8,10},{9,11},{10,... | collective-permute-start | bytes 983048 | tf_op jit(solution)/shard_map/ppermute | solution.py:30
  192.7 11.8 %collective-permute-start.13 = (bf16[32,5120]{1,0:T(8,128)(2,1)}, bf16[32,5120]{1,0:T(8,128)(2,1)}, u32[]{:S(2)}, u32[]{:S(2)}) collective-permute-start(bf16[32,5120]{1,0:T(8,128)(2,1)} %collective-permute-done.12), channel_id=1, source_target_pairs={{0,3},{1,0},{2,1},{3,2},{4,7},{5,4},{6,5},{7,6},{8,11},{9,8},{10,9... | collective-permute-start | bytes 983048 | tf_op jit(solution)/shard_map/ppermute | solution.py:30
  196.7 11.9 %collective-permute-start.10 = (bf16[64,5120]{1,0:T(8,128)(2,1)S(1)}, bf16[64,5120]{1,0:T(8,128)(2,1)S(1)}, u32[]{:S(2)}, u32[]{:S(2)}) collective-permute-start(bf16[64,5120]{1,0:T(8,128)(2,1)S(1)} %reshape.218), channel_id=1, source_target_pairs={{0,1},{1,2},{2,3},{3,0},{4,5},{5,6},{6,7},{7,4},{8,9},{9,10},{10,1... | collective-permute-start | bytes 1966088 | tf_op jit(solution)/shard_map/ppermute | solution.py:30
  196.8 21.6 %collective-permute-start.14 = (bf16[64,5120]{1,0:T(8,128)(2,1)S(1)}, bf16[64,5120]{1,0:T(8,128)(2,1)S(1)}, u32[]{:S(2)}, u32[]{:S(2)}) collective-permute-start(bf16[64,5120]{1,0:T(8,128)(2,1)S(1)} %reshape.218), channel_id=1, source_target_pairs={{0,3},{1,0},{2,1},{3,2},{4,7},{5,4},{6,5},{7,6},{8,11},{9,8},{10,9... | collective-permute-start | bytes 1966088 | tf_op jit(solution)/shard_map/ppermute | solution.py:30
  219.0 31.3 %copy-start.1 = (bf16[1280,3,320]{0,2,1:T(8,128)(2,1)S(1)}, bf16[1280,3,320]{0,2,1:T(8,128)(2,1)}, u32[]{:S(2)}) copy-start(bf16[1280,3,320]{0,2,1:T(8,128)(2,1)} %param.21) | copy-start | bytes 7372804
Sparse Core Ops, SparseCore 0:
  10.3 106.7 all-gather.1

commit v5 on v1

--- a/solution.py
+++ b/solution.py
@@ -16,14 +16,14 @@
     return centered * lax.rsqrt(spread + 1e-06) * gain
 
 
-def hidden_fold(rows, pieces):
-    up_piece, down_piece = pieces
+def hidden_half(rows, pieces):
     hidden = jax.nn.gelu(
-        jnp.dot(rows, up_piece, preferred_element_type=jnp.float32), approximate=False
+        lax.dot_general(
+            rows, pieces[0], (((1,), (1,)), ((), ())), preferred_element_type=jnp.float32
+        ),
+        approximate=False,
     ).astype(jnp.bfloat16)
-    return lax.dot_general(
-        hidden, down_piece, (((1,), (1,)), ((), ())), preferred_element_type=jnp.float32
-    )
+    return jnp.dot(hidden, pieces[1], preferred_element_type=jnp.float32)
 
 
 def permute_gather(rows, axis):
@@ -109,8 +109,8 @@
 
 
 def layer(tokens, segments, gain_attn, w_qkv, w_out, gain_mlp, w_up, w_down_t, gain_merge, w_proj):
-    both = lax.all_gather(jnp.stack([w_up, w_down_t]), ("zx", "core", "tok"), axis=2, tiled=True)
-    up_full, down_full = both[0], both[1]
+    own = lax.all_gather(jnp.stack([w_up.T, w_down_t.T]), ("zx", "tok"), axis=1, tiled=True)
+    other = lax.ppermute(own, "core", [(0, 1), (1, 0)])
     inputs = tokens.astype(jnp.float32)
     normed = layer_norm(inputs, gain_attn).astype(jnp.bfloat16)
     local_width = w_qkv.shape[2]
@@ -156,7 +156,7 @@
     )
     first = (inputs + attended).astype(jnp.bfloat16)
     normed_mlp = layer_norm(first.astype(jnp.float32), gain_mlp).astype(jnp.bfloat16)
-    mlp_out = hidden_fold(normed_mlp, (up_full, down_full))
+    mlp_out = hidden_half(normed_mlp, own) + hidden_half(normed_mlp, other)
     second = first.astype(jnp.float32) + mlp_out
     normed_merge = layer_norm(second, gain_merge).astype(jnp.bfloat16)
     merged = normed_merge.reshape(inputs.shape[0] // 4, 4 * inputs.shape[1])

time: 248 us -> 281 us (1.13)
  waiting for transfers between devices: 83.7 us -> 129 us
  local copies, waits for them, and re-layouts: 23.5 us -> 15.4 us
  other arithmetic: 28.4 us -> 20.6 us
  matrix products: 56.5 us -> 63.6 us
    all_gather x1, waiting for transfers between devices: 0.02 us -> 50.2 us  [layer(): lax.all_gather(jnp.stack([w_up.T, w_down_t.T]), ('zx', 'tok'), axis=1, ti...]
    ppermute x3, waiting for transfers between devices: 40.5 us -> 28.6 us  [permute_scatter(): lax.ppermute(outgoing, axis, [(i, (i + s) % count) for i in range(count)])]
    dynamic_slice x16, local copies, waits for them, and re-layouts: 11.2 us -> 0.12 us  [block_scores(): same = query_images[:, None] == images_blocked[kblock][None, :]]
    ppermute x6, waiting for transfers between devices: 43.2 us -> 50.1 us  [permute_gather(): lax.ppermute(rows, axis, [(i, (i + s) % count) for i in range(count)])]
    eq x16, other arithmetic: 7.35 us -> 1.92 us  [block_scores(): same = query_images[:, None] == images_blocked[kblock][None, :]]
    dot_general x8, matrix products: 14.9 us -> 20.1 us  [add_values(): jnp.einsum('hqk,khd->qhd', weights, values_blocked[kblock], preferred_ele...]
    dot_general x1 -> x2, matrix products: 25.7 us -> 27.9 us  [hidden_half(): return jnp.dot(hidden, pieces[1], preferred_element_type=jnp.float32)]
  transfers between devices with their start and end apart: 10 -> 11, of which waited for: 5 -> 8; matrix products, arithmetic and copies ran while one was open for 28% -> 25% of each run, Pallas kernels for 0% -> 0%
where the time goes in v5:
time: 281 us; the launch traced here: 280 us
  waiting for transfers between devices  129 us (46%)
  matrix products  63.6 us (23%)
  other arithmetic  20.6 us (7%)
  between operations  19.6 us (7%)
  blocking collectives  17.2 us (6%)
  local copies, waits for them, and re-layouts  15.4 us (5%)
  starting transfers between devices  13.8 us (5%)
    all_gather x1, waiting for transfers between devices, layer(): lax.all_gather(jnp.stack([w_up.T, w_down_t.T]), ('zx', 'tok'), axis=1, ti...  50.2 us
    ppermute x6, waiting for transfers between devices, permute_gather(): lax.ppermute(rows, axis, [(i, (i + s) % count) for i in range(count)])  50.1 us
    ppermute x3, waiting for transfers between devices, permute_scatter(): lax.ppermute(outgoing, axis, [(i, (i + s) % count) for i in range(count)])  28.6 us
    dot_general x2, matrix products, hidden_half(): return jnp.dot(hidden, pieces[1], preferred_element_type=jnp.float32)  27.9 us
    dot_general x8, matrix products, add_values(): jnp.einsum('hqk,khd->qhd', weights, values_blocked[kblock], preferred_ele...  20.1 us
    all_to_all x1, blocking collectives, layer(): lax.all_to_all(projected, ('zx', 'core'), split_axis=0, concat_axis=0, ti...  17.2 us
    ppermute x6, starting transfers between devices, permute_gather(): lax.ppermute(rows, axis, [(i, (i + s) % count) for i in range(count)])  8.78 us
    dot_general x1, matrix products, layer(): jnp.dot(permute_gather(merged, 'tok'), w_proj, preferred_element_type=jnp...  7.04 us
  transfers between devices with their start and end apart: 11, of which 8 were waited for; matrix products, arithmetic and copies ran while one was open for 25% of the time, Pallas kernels for 0%

profile of v5, /device:TPU:1, one launch (start us, length us, event | category | flops | bytes accessed | tf_op | source)
XLA Modules:
  0.0 280.0 jit_solution(1375399607221036362)
XLA Ops:
  6.6 1.8 pad_maximum_fusion.2
  8.4 1.3 convert_reduce_fusion.1
  9.7 1.4 fusion.108
  11.1 2.3 fusion.110
  13.3 3.7 %collective-permute-start.1 = (bf16[256,1280]{1,0:T(8,128)(2,1)}, bf16[256,1280]{1,0:T(8,128)(2,1)}, u32[]{:S(2)}, u32[]{:S(2)}) collective-permute-start(bf16[256,1280]{1,0:T(8,128)(2,1)} %fusion.110), channel_id=1, source_target_pairs={{0,2},{1,3},{2,0},{3,1},{4,6},{5,7},{6,4},{7,5},{8,10},{9,11},{10,... | collective-permute-start | bytes 1966088 | tf_op jit(solution)/shard_map/ppermute | solution.py:33
  17.5 2.3 collective-permute-start.2
  20.4 3.1 %fusion.200 = (s32[]{:T(128)}, s32[]{:T(128)}, s32[]{:T(128)}, s32[]{:T(128)}) fusion(s32[1,1024]{1,0:T(1,128)S(1)} %copy-done.6, s32[]{:T(128)} %bitcast.17, s32[]{:T(128)} %bitcast.31, s32[]{:T(128)} %bitcast.16, s32[]{:T(128)} %bitcast.32), kind=kLoop, calls=%fused_computation.249 | loop fusion | flops 12284 | bytes 4128 | tf_op jit(solution)/shard_map/reduce_sum | solution.py:71
  29.7 2.7 collective-permute-done.1
  32.4 16.4 %collective-permute-done = bf16[256,1280]{1,0:T(8,128)(2,1)} collective-permute-done((bf16[256,1280]{1,0:T(8,128)(2,1)}, bf16[256,1280]{1,0:T(8,128)(2,1)}, u32[]{:S(2)}, u32[]{:S(2)}) %collective-permute-start) | collective-permute-done | bytes 655392 | tf_op jit(solution)/shard_map/ppermute | solution.py:33
  48.8 1.8 pad_maximum_fusion
  50.8 2.7 fusion.96
  55.8 1.1 fusion.269
  57.0 1.1 copy.18
  58.0 1.2 copy.23
  60.2 3.0 %while.46 = (s32[]{:T(128)}, f32[4,512]{1,0:T(4,128)S(1)}, f32[4,512]{1,0:T(4,128)S(1)}, s32[]{:T(128)}, s32[512]{0:T(512)S(1)}, /*index=5*/s32[8,128]{1,0:T(8,1...) while((s32[]{:T(128)}, f32[4,512]{1,0:T(4,128)S(1)}, ...), condition=%wide.region_15.16_spmd, body=%wide.region_12.15_spmd.sunk | while | flops 43323396 | bytes 2748063 | solution.py:96
  63.2 50.2 %all-gather.2.cloned.1.call-done = bf16[2,2560,1280]{2,1,0:T(8,128)(2,1)} async-done(((bf16[2,40,1280]{2,1,0:T(8,128)(2,1)}), bf16[2,2560,1280]{2,1,0:T(8,128)(2,1)}) %all-gather.2.cloned.1.call-update) | async-done | bytes 13107216 | tf_op jit(solution)/shard_map/all_gather | solution.py:112
  115.2 12.8 %while.47 = (s32[]{:T(128)}, f32[512,4,80]{0,2,1:T(8,128)}, s32[]{:T(128)}, bf16[8,128,4,80]{1,3,2,0:T(8,128)(2,1)}, s32[512]{0:T(512)S(1)}, /*index=5*/s32[8,12...) while((s32[]{:T(128)}, f32[512,4,80]{0,2,1:T(8,128)}, ...), condition=%wide.region_17.18_spmd, body=%wide.region_16.17_spmd.sunk | while | flops 85426176 | bytes 2313907 | solution.py:105
  115.4 3.0 %fusion.308 = f32[512,4,80]{0,2,1:T(8,128)} fusion(f32[512,4,80]{0,2,1:T(8,128)} %get-tuple-element.625, bf16[512,4,80]{2,1,0:T(4,128)(2,1)} %get-tuple-element.644, f32[4,512]{1,0:T(4,128)S(1)} %get-tuple-element.646, f32[4,512]{1,0:T(4,128)S(1)} %get-tuple-element.645, pred[512,128]{1,0:T(8,128)(4,1)S(1)} %broadcast_compare_fusion.11, ...), kind=kOutput, calls=%fused_computation.53.clone.1 | convolution fusion | flops 85360640 | bytes 2080772 | tf_op jit(solution)/shard_map/while/body/hqk,khd->qhd/dot_general | solution.py:101
  118.6 3.0 %fusion.308 = f32[512,4,80]{0,2,1:T(8,128)} fusion(f32[512,4,80]{0,2,1:T(8,128)} %get-tuple-element.625, bf16[512,4,80]{2,1,0:T(4,128)(2,1)} %get-tuple-element.644, f32[4,512]{1,0:T(4,128)S(1)} %get-tuple-element.646, f32[4,512]{1,0:T(4,128)S(1)} %get-tuple-element.645, pred[512,128]{1,0:T(8,128)(4,1)S(1)} %broadcast_compare_fusion.11, ...), kind=kOutput, calls=%fused_computation.53.clone.1 | convolution fusion | flops 85360640 | bytes 2080772 | tf_op jit(solution)/shard_map/while/body/hqk,khd->qhd/dot_general | solution.py:101
  121.8 3.0 %fusion.308 = f32[512,4,80]{0,2,1:T(8,128)} fusion(f32[512,4,80]{0,2,1:T(8,128)} %get-tuple-element.625, bf16[512,4,80]{2,1,0:T(4,128)(2,1)} %get-tuple-element.644, f32[4,512]{1,0:T(4,128)S(1)} %get-tuple-element.646, f32[4,512]{1,0:T(4,128)S(1)} %get-tuple-element.645, pred[512,128]{1,0:T(8,128)(4,1)S(1)} %broadcast_compare_fusion.11, ...), kind=kOutput, calls=%fused_computation.53.clone.1 | convolution fusion | flops 85360640 | bytes 2080772 | tf_op jit(solution)/shard_map/while/body/hqk,khd->qhd/dot_general | solution.py:101
  125.0 3.0 %fusion.308 = f32[512,4,80]{0,2,1:T(8,128)} fusion(f32[512,4,80]{0,2,1:T(8,128)} %get-tuple-element.625, bf16[512,4,80]{2,1,0:T(4,128)(2,1)} %get-tuple-element.644, f32[4,512]{1,0:T(4,128)S(1)} %get-tuple-element.646, f32[4,512]{1,0:T(4,128)S(1)} %get-tuple-element.645, pred[512,128]{1,0:T(8,128)(4,1)S(1)} %broadcast_compare_fusion.11, ...), kind=kOutput, calls=%fused_computation.53.clone.1 | convolution fusion | flops 85360640 | bytes 2080772 | tf_op jit(solution)/shard_map/while/body/hqk,khd->qhd/dot_general | solution.py:101
  129.1 1.1 convert_element_type.92
  130.2 3.1 %while.44 = (s32[]{:T(128)}, f32[4,512]{1,0:T(4,128)S(1)}, f32[4,512]{1,0:T(4,128)S(1)}, s32[]{:T(128)}, s32[512]{0:T(512)S(1)}, /*index=5*/s32[8,128]{1,0:T(8,1...) while((s32[]{:T(128)}, f32[4,512]{1,0:T(4,128)S(1)}, ...), condition=%wide.region_7.8_spmd, body=%wide.region_4.7_spmd.sunk | while | flops 43323396 | bytes 2748063 | solution.py:96
  133.3 9.2 %while.45 = (s32[]{:T(128)}, f32[512,4,80]{0,2,1:T(8,128)S(1)}, s32[]{:T(128)}, bf16[8,128,4,80]{1,3,2,0:T(8,128)(2,1)}, s32[512]{0:T(512)S(1)}, /*index=5*/s32[...) while((s32[]{:T(128)}, f32[512,4,80]{0,2,1:T(8,128)S(1)}, ...), condition=%wide.region_9.10_spmd, body=%wide.region_8.9_spmd.sunk | while | flops 85426176 | bytes 2313907 | solution.py:105
  133.6 2.0 fusion.301
  135.9 2.0 fusion.301
  138.2 2.0 fusion.301
  140.5 2.0 fusion.301
  142.6 2.7 convolution_convert_fusion
  145.3 1.5 copy-done.3
  146.8 1.3 dynamic-slice_bitcast_fusion.10
  148.0 1.2 collective-permute-start.3
  149.2 1.5 collective-permute-start.5
  150.7 1.5 collective-permute-start.4
  152.2 13.5 %collective-permute-done.3 = bf16[256,1280]{1,0:T(8,128)(2,1)S(1)} collective-permute-done((bf16[256,1280]{1,0:T(8,128)(2,1)}, bf16[256,1280]{1,0:T(8,128)(2,1)S(1)}, u32[]{:S(2)}, u32[]{:S(2)}) %collective-permute-start.3) | collective-permute-done | bytes 655392 | tf_op jit(solution)/shard_map/ppermute | solution.py:51
  165.7 15.1 %collective-permute-done.4 = bf16[256,1280]{1,0:T(8,128)(2,1)} collective-permute-done((bf16[256,1280]{1,0:T(8,128)(2,1)S(1)}, bf16[256,1280]{1,0:T(8,128)(2,1)}, u32[]{:S(2)}, u32[]{:S(2)}) %collective-permute-start.4) | collective-permute-done | bytes 655392 | tf_op jit(solution)/shard_map/ppermute | solution.py:51
  180.9 1.8 convert_reduce_fusion
  183.0 14.2 %fusion.56 = f32[256,1280]{1,0:T(8,128)} fusion(bf16[2,2560,1280]{2,1,0:T(8,128)(2,1)} %all-gather.2.cloned.1.call-done, bf16[256,1280]{1,0:T(8,128)(2,1)S(1)} %get-tuple-element.318, f32[1280]{0:T(1024)S(1)} %copy-done.8, f32[256]{0:T(256)S(1)} %add_rsqrt_fusion.1, f32[256]{0:T(256)S(1)} %broadcast_multiply_fusion.1), kind=kOutput, calls=%fused_computation.75 | convolution fusion | flops 3399680000 | bytes 15080448 | tf_op jit(solution)/shard_map/dot_general | solution.py:26
  197.2 13.7 %fusion.272 = (f32[256]{0:T(256)S(1)}, f32[256,1280]{1,0:T(8,128)S(1)}) fusion(f32[256,1280]{1,0:T(8,128)} %fusion.56, bf16[2,2560,1280]{2,1,0:T(8,128)(2,1)} %collective-permute-done.6, bf16[256,1280]{1,0:T(8,128)(2,1)S(1)} %get-tuple-element.318, f32[1280]{0:T(1024)S(1)} %copy-done.8, f32[256]{0:T(256)S(1)} %add_rsqrt_fusion.1, ...), kind=kOutput, calls=%fused_computation.326 | convolution fusion | flops 3400990464 | bytes 17050624 | tf_op jit(solution)/shard_map/dot_general | solution.py:26
  211.5 1.2 reshape.214
  212.7 1.2 collective-permute-start.9
  213.9 1.2 collective-permute-start.8
  215.5 12.9 %collective-permute-done.9 = bf16[64,5120]{1,0:T(8,128)(2,1)S(1)} collective-permute-done((bf16[64,5120]{1,0:T(8,128)(2,1)}, bf16[64,5120]{1,0:T(8,128)(2,1)S(1)}, u32[]{:S(2)}, u32[]{:S(2)}) %collective-permute-start.9) | collective-permute-done | bytes 655392 | tf_op jit(solution)/shard_map/ppermute | solution.py:33
  228.4 2.0 collective-permute-done.8
  230.4 16.0 %collective-permute-done.7 = bf16[64,5120]{1,0:T(8,128)(2,1)} collective-permute-done((bf16[64,5120]{1,0:T(8,128)(2,1)}, bf16[64,5120]{1,0:T(8,128)(2,1)}, u32[]{:S(2)}, u32[]{:S(2)}) %collective-permute-start.7) | collective-permute-done | bytes 655392 | tf_op jit(solution)/shard_map/ppermute | solution.py:33
  246.4 1.4 pad_maximum_fusion.1
  248.0 7.0 %fusion.177 = bf16[32,8,1024]{2,1,0:T(8,128)(2,1)S(1)} fusion(bf16[5120,1024]{1,0:T(8,128)(2,1)} %param.27, bf16[64,5120]{1,0:T(8,128)(2,1)S(1)} %get-tuple-element.324, bf16[64,5120]{1,0:T(8,128)(2,1)S(1)} %get-tuple-element.325, bf16[64,5120]{1,0:T(8,128)(2,1)S(1)} %get-tuple-element.326, bf16[64,5120]{1,0:T(8,128)(2,1)S(1)} %get-tuple-element.323), kind=kOutput, calls=%fused_computation.220 | convolution fusion | flops 2695102464 | bytes 13631488 | tf_op jit(solution)/shard_map/dot_general | solution.py:163
  255.1 17.2 %all_to_all.12 = bf16[32,8,1024]{2,1,0:T(8,128)(2,1)S(1)} all-to-all(bf16[32,8,1024]{2,1,0:T(8,128)(2,1)S(1)} %fusion.177), channel_id=1, replica_groups=mesh['zx'=16,'core'=2,'tok'=4] {'zx','core'}, dimensions={0} | all-to-all | bytes 1048576 | tf_op jit(solution)/shard_map/all_to_all | solution.py:168
  (134 shorter events, 17.1 us)
Async XLA Ops:
  6.5 44.3 %copy-start = (bf16[1280,3,320]{0,2,1:T(8,128)(2,1)S(1)}, bf16[1280,3,320]{0,2,1:T(8,128)(2,1)}, u32[]{:S(2)}) copy-start(bf16[1280,3,320]{0,2,1:T(8,128)(2,1)} %param.21) | copy-start | bytes 7372804
  6.5 22.8 %copy-start.2 = (bf16[256,1280]{1,0:T(8,128)(2,1)S(1)}, bf16[256,1280]{1,0:T(8,128)(2,1)}, u32[]{:S(2)}) copy-start(bf16[256,1280]{1,0:T(8,128)(2,1)} %param.18) | copy-start | bytes 1966084
  6.5 22.9 %copy-start.5 = (f32[1280]{0:T(1024)S(1)}, f32[1280]{0:T(1024)}, u32[]{:S(2)}) copy-start(f32[1280]{0:T(1024)} %param.20) | copy-start | bytes 15364
  6.5 13.2 %copy-start.6 = (s32[1,1024]{1,0:T(1,128)S(1)}, s32[1,1024]{1,0:T(1,128)}, u32[]{:S(2)}) copy-start(s32[1,1024]{1,0:T(1,128)} %param.19) | copy-start | bytes 12292
  6.5 106.9 %all-gather.2.cloned.1.call-start = ((), (), s32[]{:S(2)}) async-start(), calls=%async_computation.1 | async-start | bytes 13312000 | tf_op jit(solution)/shard_map/all_gather | solution.py:112
  13.3 19.0 %collective-permute-start.1 = (bf16[256,1280]{1,0:T(8,128)(2,1)}, bf16[256,1280]{1,0:T(8,128)(2,1)}, u32[]{:S(2)}, u32[]{:S(2)}) collective-permute-start(bf16[256,1280]{1,0:T(8,128)(2,1)} %fusion.110), channel_id=1, source_target_pairs={{0,2},{1,3},{2,0},{3,1},{4,6},{5,7},{6,4},{7,5},{8,10},{9,11},{10,... | collective-permute-start | bytes 1966088 | tf_op jit(solution)/shard_map/ppermute | solution.py:33
  17.1 31.7 %collective-permute-start = (bf16[256,1280]{1,0:T(8,128)(2,1)}, bf16[256,1280]{1,0:T(8,128)(2,1)}, u32[]{:S(2)}, u32[]{:S(2)}) collective-permute-start(bf16[256,1280]{1,0:T(8,128)(2,1)} %fusion.110), channel_id=1, source_target_pairs={{0,1},{1,2},{2,3},{3,0},{4,5},{5,6},{6,7},{7,4},{8,9},{9,10},{10,1... | collective-permute-start | bytes 1966088 | tf_op jit(solution)/shard_map/ppermute | solution.py:33
  17.5 31.3 %collective-permute-start.2 = (bf16[256,1280]{1,0:T(8,128)(2,1)}, bf16[256,1280]{1,0:T(8,128)(2,1)}, u32[]{:S(2)}, u32[]{:S(2)}) collective-permute-start(bf16[256,1280]{1,0:T(8,128)(2,1)} %fusion.110), channel_id=1, source_target_pairs={{0,3},{1,0},{2,1},{3,2},{4,7},{5,4},{6,5},{7,6},{8,11},{9,8},{10,9... | collective-permute-start | bytes 1966088 | tf_op jit(solution)/shard_map/ppermute | solution.py:33
  53.6 1.5 copy-start.4
  113.5 83.7 %collective-permute-start.6 = (bf16[2,2560,1280]{2,1,0:T(8,128)(2,1)}, bf16[2,2560,1280]{2,1,0:T(8,128)(2,1)}, u32[]{:S(2)}, u32[]{:S(2)}) collective-permute-start(bf16[2,2560,1280]{2,1,0:T(8,128)(2,1)} %all-gather.2.cloned.1.call-done), channel_id=1, source_target_pairs={{0,4},{4,0},{1,5},{5,1},{2,6},{6,2},{3,7},{7,3},{8,12},{12,8},{9,1... | collective-permute-start | bytes 39321608 | tf_op jit(solution)/shard_map/ppermute | solution.py:113
  145.3 1.5 copy-start.3
  148.0 35.0 %copy-start.8 = (f32[1280]{0:T(1024)S(1)}, f32[1280]{0:T(1024)}, u32[]{:S(2)}) copy-start(f32[1280]{0:T(1024)} %param.23) | copy-start | bytes 15364
  148.0 17.7 %collective-permute-start.3 = (bf16[256,1280]{1,0:T(8,128)(2,1)}, bf16[256,1280]{1,0:T(8,128)(2,1)S(1)}, u32[]{:S(2)}, u32[]{:S(2)}) collective-permute-start(bf16[256,1280]{1,0:T(8,128)(2,1)} %get-tuple-element.327), channel_id=1, source_target_pairs={{0,1},{1,2},{2,3},{3,0},{4,5},{5,6},{6,7},{7,4},{8,9},{9,10},{10,1... | collective-permute-start | bytes 1966088 | tf_op jit(solution)/shard_map/ppermute | solution.py:51
  149.2 16.5 %collective-permute-start.5 = (bf16[256,1280]{1,0:T(8,128)(2,1)}, bf16[256,1280]{1,0:T(8,128)(2,1)S(1)}, u32[]{:S(2)}, u32[]{:S(2)}) collective-permute-start(bf16[256,1280]{1,0:T(8,128)(2,1)} %get-tuple-element.328), channel_id=1, source_target_pairs={{0,3},{1,0},{2,1},{3,2},{4,7},{5,4},{6,5},{7,6},{8,11},{9,8},{10,9... | collective-permute-start | bytes 1966088 | tf_op jit(solution)/shard_map/ppermute | solution.py:51
  150.7 30.1 %collective-permute-start.4 = (bf16[256,1280]{1,0:T(8,128)(2,1)S(1)}, bf16[256,1280]{1,0:T(8,128)(2,1)}, u32[]{:S(2)}, u32[]{:S(2)}) collective-permute-start(bf16[256,1280]{1,0:T(8,128)(2,1)S(1)} %get-tuple-element.329), channel_id=1, source_target_pairs={{0,2},{1,3},{2,0},{3,1},{4,6},{5,7},{6,4},{7,5},{8,10},{9,11},{10,... | collective-permute-start | bytes 1966088 | tf_op jit(solution)/shard_map/ppermute | solution.py:51
  197.2 14.0 %copy-start.7 = (f32[1280]{0:T(1024)S(1)}, f32[1280]{0:T(1024)}, u32[]{:S(2)}) copy-start(f32[1280]{0:T(1024)} %param.26) | copy-start | bytes 15364
  212.7 15.6 %collective-permute-start.9 = (bf16[64,5120]{1,0:T(8,128)(2,1)}, bf16[64,5120]{1,0:T(8,128)(2,1)S(1)}, u32[]{:S(2)}, u32[]{:S(2)}) collective-permute-start(bf16[64,5120]{1,0:T(8,128)(2,1)} %reshape.214), channel_id=1, source_target_pairs={{0,3},{1,0},{2,1},{3,2},{4,7},{5,4},{6,5},{7,6},{8,11},{9,8},{10,9... | collective-permute-start | bytes 1966088 | tf_op jit(solution)/shard_map/ppermute | solution.py:33
  213.9 16.5 %collective-permute-start.8 = (bf16[64,5120]{1,0:T(8,128)(2,1)}, bf16[64,5120]{1,0:T(8,128)(2,1)S(1)}, u32[]{:S(2)}, u32[]{:S(2)}) collective-permute-start(bf16[64,5120]{1,0:T(8,128)(2,1)} %reshape.214), channel_id=1, source_target_pairs={{0,2},{1,3},{2,0},{3,1},{4,6},{5,7},{6,4},{7,5},{8,10},{9,11},{10,... | collective-permute-start | bytes 1966088 | tf_op jit(solution)/shard_map/ppermute | solution.py:33
  215.1 31.3 %collective-permute-start.7 = (bf16[64,5120]{1,0:T(8,128)(2,1)}, bf16[64,5120]{1,0:T(8,128)(2,1)}, u32[]{:S(2)}, u32[]{:S(2)}) collective-permute-start(bf16[64,5120]{1,0:T(8,128)(2,1)} %reshape.214), channel_id=1, source_target_pairs={{0,1},{1,2},{2,3},{3,0},{4,5},{5,6},{6,7},{7,4},{8,9},{9,10},{10,1... | collective-permute-start | bytes 1966088 | tf_op jit(solution)/shard_map/ppermute | solution.py:33
  248.0 25.1 %copy-start.1 = (bf16[1280,3,320]{0,2,1:T(8,128)(2,1)S(1)}, bf16[1280,3,320]{0,2,1:T(8,128)(2,1)}, u32[]{:S(2)}) copy-start(bf16[1280,3,320]{0,2,1:T(8,128)(2,1)} %param.21) | copy-start | bytes 7372804
Sparse Core Ops, SparseCore 0:
  10.2 103.1 all-gather.1
